TPU v7x, 512 devices: a whole 4x8x8 slice. The times are simulated.
512 devices in a mesh: box: 64 (over x, y, z_hi), row: 8 (over z_lo, core).
Axes of the slice: x: 4, y: 8, z: 8 (z_hi: 2, z_lo: 4; z = z_hi * 4 + z_lo), core: 2. Of those that a mesh axis runs over, the one named last changes fastest.
Arguments:
- leaf_maps: float32 [64, 2048, 2048], P('box', 'row'), as said below
- iface_index: int32 [64, 512], replicated, may hold values from 0 to 511, as said below
Outputs:
- merged_maps: bfloat16 [64, 2048, 3072], P('box', 'row')
Inputs may be any that keep to these rules, and one draw needn't show every extreme that they name: Each row of iface_index is a permutation of 0 .. 511. Each leaf_maps[c] is exactly symmetric.
All inputs are finite; a program needn't handle non-finite values.
Results may differ from a plain program's by a relative error of at most 0.001.
Values sent between devices are 32-bit elements; how exact they have to be, the bound alone decides.
No kernel may reach another device: no remote copies, remote signals or barrier semaphores. Data moves between devices by JAX's collectives and lax.ppermute only.
A program may use at most 64 MiB of HBM per device.

v0:
```python
import jax
import jax.numpy as jnp
from jax import lax
from jax.experimental import pallas as pl
from jax.experimental.pallas import tpu as pltpu
from jax.sharding import PartitionSpec as P

AXES = ("box", "row")
HI = lax.Precision.HIGHEST


def _gj_kernel(a_ref, o_ref, p_ref):
    n = a_ref.shape[0]
    nb = p_ref.shape[0]
    o_ref[...] = a_ref[...]
    lane_p = lax.broadcasted_iota(jnp.int32, (nb, nb), 1)
    lane_r = lax.broadcasted_iota(jnp.int32, (1, nb), 1)
    sub_c = lax.broadcasted_iota(jnp.int32, (nb, 1), 0)
    for kb in range(n // nb):
        lo = kb * nb
        p_ref[...] = o_ref[lo:lo + nb, lo:lo + nb]

        def step(j, carry):
            block = p_ref[...]
            row = p_ref[pl.ds(j, 1), :]
            piv = jnp.sum(jnp.where(lane_r == j, row, 0.0), axis=1, keepdims=True)
            inv = 1.0 / piv
            rnew = jnp.where(lane_r == j, 1.0, row) * inv
            col = jnp.sum(jnp.where(lane_p == j, block, 0.0), axis=1, keepdims=True)
            col = jnp.where(sub_c == j, 0.0, col)
            p_ref[...] = jnp.where(lane_p == j, 0.0, block) - col * rnew
            p_ref[pl.ds(j, 1), :] = rnew
            return carry

        lax.fori_loop(0, nb, step, 0)
        pinv = p_ref[...]
        lane_n = lax.broadcasted_iota(jnp.int32, (nb, n), 1)
        sub_n = lax.broadcasted_iota(jnp.int32, (nb, n), 0)
        in_cols = jnp.logical_and(lane_n >= lo, lane_n < lo + nb)
        eye = jnp.where(lane_n - lo == sub_n, 1.0, 0.0)
        rows = jnp.where(in_cols, eye, o_ref[lo:lo + nb, :])
        rnew = jnp.dot(pinv, rows, precision=HI, preferred_element_type=jnp.float32)
        sub_k = lax.broadcasted_iota(jnp.int32, (n, nb), 0)
        cols = jnp.where(jnp.logical_and(sub_k >= lo, sub_k < lo + nb), 0.0, o_ref[:, lo:lo + nb])
        lane_a = lax.broadcasted_iota(jnp.int32, (n, n), 1)
        whole = jnp.where(jnp.logical_and(lane_a >= lo, lane_a < lo + nb), 0.0, o_ref[...])
        o_ref[...] = whole - jnp.dot(cols, rnew, precision=HI, preferred_element_type=jnp.float32)
        o_ref[lo:lo + nb, :] = rnew


def spd_inverse(a, nb=128):
    n = a.shape[0]
    return pl.pallas_call(
        _gj_kernel,
        out_shape=jax.ShapeDtypeStruct((n, n), jnp.float32),
        in_specs=[pl.BlockSpec(memory_space=pltpu.VMEM)],
        out_specs=pl.BlockSpec(memory_space=pltpu.VMEM),
        scratch_shapes=[pltpu.VMEM((nb, nb), jnp.float32)],
        cost_estimate=pl.CostEstimate(flops=2 * n * n * n * 6, bytes_accessed=8 * n * n, transcendentals=0),
    )(a)


def ring_pairs(nbox, nrow, shift):
    span = 2 * nrow
    chips = nrow
    pairs = []
    for g in range(nbox * nrow):
        p, q = divmod(g, span)
        z, c = divmod(q, 2)
        pairs.append((g, p * span + 2 * ((z + shift) % chips) + c))
    return pairs


def ring_gather(mine, nbox, nrow):
    chips = nrow
    cw = ring_pairs(nbox, nrow, 1)
    ccw = ring_pairs(nbox, nrow, -1)
    swap = [(g, g ^ 1) for g in range(nbox * nrow)]
    rows = mine.shape[0]
    rel = [None] * chips
    rel[0] = mine
    a = mine
    b = mine
    half = chips // 2
    for k in range(1, (chips - 1) // 2 + 1):
        a = lax.ppermute(a, AXES, cw)
        b = lax.ppermute(b, AXES, ccw)
        rel[k] = a
        rel[chips - k] = b
    if chips % 2 == 0:
        top = lax.ppermute(a[: rows // 2], AXES, cw)
        bot = lax.ppermute(b[rows // 2 :], AXES, ccw)
        rel[half] = jnp.concatenate([top, bot], 0)
    sib = [lax.ppermute(piece, AXES, swap) for piece in rel]
    stacked = jnp.stack(rel + sib)
    q = lax.axis_index("row") + nrow * (lax.axis_index("box") % 2)
    z = q // 2
    c = q % 2
    zs = jnp.arange(chips, dtype=jnp.int32)
    offset = (z - zs) % chips
    idx = jnp.stack([offset + chips * c, offset + chips * (1 - c)], 1).reshape(-1)
    full = jnp.take(stacked, idx, axis=0)
    return full.reshape(chips, 2 * rows, mine.shape[1])


def body(leaf_maps, iface_index):
    local = leaf_maps[0]
    rows_here = local.shape[0]
    width = local.shape[1]
    inner = iface_index.shape[1]
    outer = width - inner
    nbox = lax.axis_size("box")
    nrow = lax.axis_size("row")
    box_id = lax.axis_index("box")
    is_first = box_id % 2 == 0
    first_id = box_id - box_id % 2
    own_index = lax.dynamic_index_in_dim(iface_index, box_id, 0, keepdims=False)
    index_a = lax.dynamic_index_in_dim(iface_index, first_id, 0, keepdims=False)
    index_b = lax.dynamic_index_in_dim(iface_index, first_id + 1, 0, keepdims=False)
    mine = jnp.take(local[:, outer:], own_index, axis=1)
    full = ring_gather(mine, nbox, nrow)
    chips = full.shape[0]
    g_a = full[: chips // 2].reshape(width, inner)
    g_b = full[chips // 2 :].reshape(width, inner)
    schur = jnp.take(g_a[outer:], index_a, axis=0) + jnp.take(g_b[outer:], index_b, axis=0)
    squared = jnp.dot(schur, schur, precision=HI)
    sinv = jnp.dot(spd_inverse(squared), schur, precision=HI)
    first_ext = g_a[:outer]
    second_ext = g_b[:outer]
    global_rows = lax.axis_index("row") * rows_here + jnp.arange(rows_here, dtype=jnp.int32)
    unit = (own_index[None, :] == (global_rows - outer)[:, None]).astype(jnp.float32)
    replaced = jnp.logical_and(is_first, global_rows >= outer)
    left = jnp.where(replaced[:, None], unit, mine)
    local_ext = local[:, :outer]
    zero = jnp.zeros((), jnp.float32)
    left_part = jnp.where(jnp.logical_and(is_first, global_rows < outer)[:, None], local_ext, zero)
    right_part = jnp.where(is_first, zero, local_ext)
    base = jnp.concatenate([left_part, right_part], 1)
    solved = jnp.dot(left, sinv, precision=HI)
    contract = (((1,), (1,)), ((), ()))
    update_first = lax.dot_general(solved, first_ext, contract, precision=lax.Precision.HIGHEST)
    update_second = lax.dot_general(solved, second_ext, contract, precision=lax.Precision.HIGHEST)
    merged = base - jnp.concatenate([update_first, update_second], 1)
    return merged.astype(jnp.bfloat16)[None]


def solution(mesh):
    in_specs = (P("box", "row", None), P())
    out_specs = P("box", "row", None)
    return jax.shard_map(body, mesh=mesh, in_specs=in_specs, out_specs=out_specs, check_vma=False)
```

profile of v0, /device:TPU:1, one launch (start us, length us, event | category | flops | bytes accessed | tf_op | source)
XLA Modules:
  0.0 194.0 jit_solution(7555514695001465407)
XLA Ops:
  0.0 0.9 compare_select_fusion
  0.9 1.1 slice.65
  2.0 0.2 copy.9
  2.2 1.6 gather_fusion
  3.8 0.1 bitcast_select_fusion.1
  3.9 4.8 %collective-permute-start = (f32[256,512]{0,1:T(8,128)S(1)}, f32[256,512]{0,1:T(8,128)}, u32[]{:S(2)}, u32[]{:S(2)}) collective-permute-start(f32[256,512]{0,1:T(8,128)S(1)} %bitcast_select_fusion.1), channel_id=1, source_target_pairs={{0,2},{1,3},{2,4},{3,5},{4,6},{5,7},{6,8},{7,9},{8,10},{9,11},{10,... | collective-permute-start | bytes 1572872 | tf_op jit(solution)/shard_map/ppermute | solution.py:86
  8.7 8.6 %collective-permute-start.4 = (f32[256,512]{0,1:T(8,128)S(1)}, f32[256,512]{0,1:T(8,128)}, u32[]{:S(2)}, u32[]{:S(2)}) collective-permute-start(f32[256,512]{0,1:T(8,128)S(1)} %bitcast_select_fusion.1), channel_id=1, source_target_pairs={{0,14},{1,15},{2,0},{3,1},{4,2},{5,3},{6,4},{7,5},{8,6},{9,7},{10,... | collective-permute-start | bytes 1572872 | tf_op jit(solution)/shard_map/ppermute | solution.py:87
  17.3 2.9 %collective-permute-start.8 = (f32[256,512]{0,1:T(8,128)S(1)}, f32[256,512]{0,1:T(8,128)}, u32[]{:S(2)}, u32[]{:S(2)}) collective-permute-start(f32[256,512]{0,1:T(8,128)S(1)} %bitcast_select_fusion.1), channel_id=1, source_target_pairs={{0,1},{1,0},{2,3},{3,2},{4,5},{5,4},{6,7},{7,6},{8,9},{9,8},{10,11... | collective-permute-start | bytes 1572872 | tf_op jit(solution)/shard_map/ppermute | solution.py:94
  20.3 0.8 constant_dynamic-slice_fusion.1
  21.1 1.9 select_bitcast_fusion.1
  23.0 0.1 copy.10
  23.1 0.1 reshape.235
  23.2 3.9 %collective-permute-done = f32[256,512]{0,1:T(8,128)} collective-permute-done((f32[256,512]{0,1:T(8,128)S(1)}, f32[256,512]{0,1:T(8,128)}, u32[]{:S(2)}, u32[]{:S(2)}) %collective-permute-start) | collective-permute-done | bytes 524320 | tf_op jit(solution)/shard_map/ppermute | solution.py:86
  27.1 1.9 collective-permute-start.1
  29.1 0.1 reshape.234
  29.1 0.0 collective-permute-done.4
  29.1 4.6 %collective-permute-start.5 = (f32[256,512]{0,1:T(8,128)}, f32[256,512]{0,1:T(8,128)S(1)}, u32[]{:S(2)}, u32[]{:S(2)}) collective-permute-start(f32[256,512]{0,1:T(8,128)} %collective-permute-done.4), channel_id=1, source_target_pairs={{0,14},{1,15},{2,0},{3,1},{4,2},{5,3},{6,4},{7,5},{8,6},{9,7},{10,... | collective-permute-start | bytes 1572872 | tf_op jit(solution)/shard_map/ppermute | solution.py:87
  33.7 0.9 fusion.1
  34.7 8.0 %collective-permute-done.1 = f32[256,512]{0,1:T(8,128)S(1)} collective-permute-done((f32[256,512]{0,1:T(8,128)}, f32[256,512]{0,1:T(8,128)S(1)}, u32[]{:S(2)}, u32[]{:S(2)}) %collective-permute-start.1) | collective-permute-done | bytes 524320 | tf_op jit(solution)/shard_map/ppermute | solution.py:86
  42.7 1.9 collective-permute-start.2
  44.6 0.0 collective-permute-done.5
  44.6 4.6 %collective-permute-start.6 = (f32[256,512]{0,1:T(8,128)S(1)}, f32[256,512]{0,1:T(8,128)S(1)}, u32[]{:S(2)}, u32[]{:S(2)}) collective-permute-start(f32[256,512]{0,1:T(8,128)S(1)} %collective-permute-done.5), channel_id=1, source_target_pairs={{0,14},{1,15},{2,0},{3,1},{4,2},{5,3},{6,4},{7,5},{8,6},{9,7},{10,... | collective-permute-start | bytes 1572872 | tf_op jit(solution)/shard_map/ppermute | solution.py:87
  49.2 4.6 %collective-permute-start.9 = (f32[256,512]{0,1:T(8,128)}, f32[256,512]{0,1:T(8,128)S(1)}, u32[]{:S(2)}, u32[]{:S(2)}) collective-permute-start(f32[256,512]{0,1:T(8,128)} %collective-permute-done), channel_id=1, source_target_pairs={{0,1},{1,0},{2,3},{3,2},{4,5},{5,4},{6,7},{7,6},{8,9},{9,8},{10,11... | collective-permute-start | bytes 1572872 | tf_op jit(solution)/shard_map/ppermute | solution.py:94
  53.8 1.9 collective-permute-start.15
  55.7 1.9 bitcast_dynamic-update-slice_fusion.14
  57.6 1.9 collective-permute-start.3
  59.6 0.8 bitcast_dynamic-update-slice_fusion.13
  60.4 4.6 %collective-permute-start.7 = (f32[128,512]{0,1:T(8,128)S(1)}, f32[128,512]{0,1:T(8,128)S(1)}, u32[]{:S(2)}, u32[]{:S(2)}) collective-permute-start(f32[128,512]{0,1:T(8,128)S(1)} %slice.67), channel_id=1, source_target_pairs={{0,14},{1,15},{2,0},{3,1},{4,2},{5,3},{6,4},{7,5},{8,6},{9,7},{10,... | collective-permute-start | bytes 786440 | tf_op jit(solution)/shard_map/ppermute | solution.py:92
  65.0 0.8 bitcast_dynamic-update-slice_fusion.12
  65.8 0.1 collective-permute-done.3
  66.0 5.5 %collective-permute-start.10 = (f32[256,512]{0,1:T(8,128)S(1)}, f32[256,512]{0,1:T(8,128)S(1)}, u32[]{:S(2)}, u32[]{:S(2)}) collective-permute-start(f32[256,512]{0,1:T(8,128)S(1)} %collective-permute-done.1), channel_id=1, source_target_pairs={{0,1},{1,0},{2,3},{3,2},{4,5},{5,4},{6,7},{7,6},{8,9},{9,8},{10,11... | collective-permute-start | bytes 1572872 | tf_op jit(solution)/shard_map/ppermute | solution.py:94
  71.5 2.3 %collective-permute-start.14 = (f32[256,512]{0,1:T(8,128)S(1)}, f32[256,512]{0,1:T(8,128)S(1)}, u32[]{:S(2)}, u32[]{:S(2)}) collective-permute-start(f32[256,512]{0,1:T(8,128)S(1)} %collective-permute-done.5), channel_id=1, source_target_pairs={{0,1},{1,0},{2,3},{3,2},{4,5},{5,4},{6,7},{7,6},{8,9},{9,8},{10,11... | collective-permute-start | bytes 1572872 | tf_op jit(solution)/shard_map/ppermute | solution.py:94
  73.9 0.8 bitcast_dynamic-update-slice_fusion.11
  74.7 0.8 bitcast_dynamic-update-slice_fusion.10
  75.5 0.8 bitcast_dynamic-update-slice_fusion.9
  76.4 1.9 bitcast_dynamic-update-slice_fusion.8
  78.2 2.0 %collective-permute-start.11 = (f32[256,512]{0,1:T(8,128)S(1)}, f32[256,512]{0,1:T(8,128)S(1)}, u32[]{:S(2)}, u32[]{:S(2)}) collective-permute-start(f32[256,512]{0,1:T(8,128)S(1)} %collective-permute-done.2), channel_id=1, source_target_pairs={{0,1},{1,0},{2,3},{3,2},{4,5},{5,4},{6,7},{7,6},{8,9},{9,8},{10,11... | collective-permute-start | bytes 1572872 | tf_op jit(solution)/shard_map/ppermute | solution.py:94
  80.3 1.9 bitcast_dynamic-update-slice_fusion.7
  82.2 2.3 %collective-permute-start.12 = (f32[256,512]{0,1:T(8,128)S(1)}, f32[256,512]{0,1:T(8,128)S(1)}, u32[]{:S(2)}, u32[]{:S(2)}) collective-permute-start(f32[256,512]{0,1:T(8,128)S(1)} %constant_dynamic-update-slice_fusion), channel_id=1, source_target_pairs={{0,1},{1,0},{2,3},{3,2},{4,5},{5,4},{6,7},{7,6},{8,9},{9,8},{10,11... | collective-permute-start | bytes 1572872 | tf_op jit(solution)/shard_map/ppermute | solution.py:94
  84.4 0.8 bitcast_dynamic-update-slice_fusion.6
  85.3 2.0 %collective-permute-start.13 = (f32[256,512]{0,1:T(8,128)S(1)}, f32[256,512]{0,1:T(8,128)S(1)}, u32[]{:S(2)}, u32[]{:S(2)}) collective-permute-start(f32[256,512]{0,1:T(8,128)S(1)} %collective-permute-done.6), channel_id=1, source_target_pairs={{0,1},{1,0},{2,3},{3,2},{4,5},{5,4},{6,7},{7,6},{8,9},{9,8},{10,11... | collective-permute-start | bytes 1572872 | tf_op jit(solution)/shard_map/ppermute | solution.py:94
  87.3 0.8 bitcast_dynamic-update-slice_fusion.5
  88.2 0.8 bitcast_dynamic-update-slice_fusion.4
  89.0 0.8 bitcast_dynamic-update-slice_fusion.3
  89.9 0.8 bitcast_dynamic-update-slice_fusion.2
  90.7 0.8 bitcast_dynamic-update-slice_fusion.1
  91.5 0.9 bitcast_dynamic-update-slice_fusion
  92.4 7.7 %gather_fusion.1 = f32[16,256,512]{1,2,0:T(8,128)} fusion(f32[16,256,512]{1,2,0:T(8,128)} %bitcast_dynamic-update-slice_fusion, s32[1024]{0:T(1024)S(1)} %pad_clamp_fusion.2), kind=kCustom, calls=%fused_computation.3 | custom fusion | bytes 16777280 | tf_op jit(solution)/shard_map/jit(_take)/gather | solution.py:102
  100.1 4.2 %broadcast_select_fusion = f32[16,256,512]{1,2,0:T(8,128)S(1)} fusion(f32[16,256,512]{1,2,0:T(8,128)} %gather_fusion.1, pred[16]{0:T(512)(128)(4,1)S(1)} %compare_and_fusion.2), kind=kLoop, calls=%fused_computation.4 | loop fusion | flops 2097152 | bytes 16777232 | tf_op jit(solution)/shard_map/jit(_take)/select_n | solution.py:102
  104.4 0.1 fusion.15
  104.5 3.0 %fusion.14 = (f32[6,256,512]{1,2,0:T(8,128)}, f32[6,256,512]{1,2,0:T(8,128)}) fusion(f32[16,256,512]{1,2,0:T(8,128)S(1)} %broadcast_select_fusion), kind=kLoop, calls=%fused_computation.70 | loop fusion | bytes 12582912 | tf_op jit(solution)/shard_map/slice | solution.py:128
  107.5 0.3 copy.12
  107.8 0.3 copy.13
  108.2 1.8 gather_fusion.2
  110.0 1.6 gather_fusion.3
  111.6 3.1 %fusion.13.a_ref = f32[512,512]{1,0:T(8,128)} fusion(f32[512,512]{1,0:T(8,128)S(1)} %gather_fusion.3, f32[512,512]{1,0:T(8,128)S(1)} %gather_fusion.2, pred[512]{0:T(512)(128)(4,1)S(1)} %get-tuple-element.22, pred[512]{0:T(512)(128)(4,1)S(1)} %get-tuple-element.23), kind=kOutput, calls=%fused_computation.69 | convolution fusion | flops 1611399168 | bytes 3146752 | tf_op jit(solution)/shard_map/dot_general | solution.py:126
  114.7 59.1 %shard_map.28 = f32[512,512]{1,0:T(8,128)} custom-call(f32[512,512]{1,0:T(8,128)} %fusion.13.a_ref), custom_call_target="tpu_custom_call" | custom-call | flops 1610612736 | bytes 2097152 | tf_op jit(solution)/shard_map/pallas_call | solution.py:53
  173.9 4.2 %fusion.12 = f32[512,512]{1,0:T(8,128)} fusion(f32[512,512]{1,0:T(8,128)} %shard_map.28, f32[512,512]{1,0:T(8,128)S(1)} %gather_fusion.3, f32[512,512]{1,0:T(8,128)S(1)} %gather_fusion.2, pred[512]{0:T(512)(128)(4,1)S(1)} %get-tuple-element.22, pred[512]{0:T(512)(128)(4,1)S(1)} %get-tuple-element.23), kind=kOutput, calls=%fused_computation.68 | convolution fusion | flops 1611399168 | bytes 4195328 | tf_op jit(solution)/shard_map/dot_general | solution.py:127
  178.1 2.4 %copy.14 = f32[6,256,512]{2,1,0:T(8,128)S(1)} copy(f32[6,256,512]{1,2,0:T(8,128)} %get-tuple-element.8) | data formatting | bytes 6291456 | tf_op jit(solution)/shard_map/slice | solution.py:128
  180.5 3.6 %copy.15 = f32[6,256,512]{2,1,0:T(8,128)} copy(f32[6,256,512]{1,2,0:T(8,128)} %get-tuple-element.9) | data formatting | bytes 6291456 | tf_op jit(solution)/shard_map/slice | solution.py:129
  184.1 2.7 %fusion.2 = f32[256,512]{1,0:T(8,128)S(1)} fusion(f32[512,512]{1,0:T(8,128)} %fusion.12, f32[256,512]{0,1:T(8,128)} %copy-done.4, s32[256]{0:T(256)S(1)} %fusion.9, s32[512]{0:T(512)S(1)} %bitcast.71, pred[256]{0:T(512)(128)(4,1)S(1)} %get-tuple-element.20), kind=kOutput, calls=%fused_computation.30 | convolution fusion | flops 805699584 | bytes 2100480 | tf_op jit(solution)/shard_map/dot_general | solution.py:139
  186.8 2.8 %convolution_bitcast_fusion.1 = f32[1,256,1536]{2,1,0:T(8,128)S(1)} fusion(f32[256,512]{1,0:T(8,128)S(1)} %fusion.2, f32[1536,512]{1,0:T(8,128)S(1)} %bitcast.66), kind=kOutput, calls=%fused_computation.8 | convolution fusion | flops 2415919104 | bytes 5242880 | tf_op jit(solution)/shard_map/dot_general | solution.py:141
  189.6 2.8 %convolution_bitcast_fusion = f32[1,256,1536]{2,1,0:T(8,128)S(1)} fusion(f32[256,512]{1,0:T(8,128)S(1)} %fusion.2, f32[1536,512]{1,0:T(8,128)S(1)} %bitcast.67), kind=kOutput, calls=%fused_computation.7 | convolution fusion | flops 2415919104 | bytes 5242880 | tf_op jit(solution)/shard_map/dot_general | solution.py:142
  192.5 1.5 fusion
  (38 shorter events, 0.2 us)
Async XLA Ops:
  0.0 21.1 %copy-start.3 = (f32[1,256,2048]{2,1,0:T(8,128)S(1)}, f32[1,256,2048]{2,1,0:T(8,128)}, u32[]{:S(2)}) copy-start(f32[1,256,2048]{2,1,0:T(8,128)} %param.4) | copy-start | bytes 6291460
  3.9 81.4 %copy-start.4 = (f32[256,512]{0,1:T(8,128)}, f32[256,512]{0,1:T(8,128)S(1)}, u32[]{:S(2)}) copy-start(f32[256,512]{0,1:T(8,128)S(1)} %bitcast_select_fusion.1) | copy-start | bytes 1572868
  3.9 23.2 %collective-permute-start = (f32[256,512]{0,1:T(8,128)S(1)}, f32[256,512]{0,1:T(8,128)}, u32[]{:S(2)}, u32[]{:S(2)}) collective-permute-start(f32[256,512]{0,1:T(8,128)S(1)} %bitcast_select_fusion.1), channel_id=1, source_target_pairs={{0,2},{1,3},{2,4},{3,5},{4,6},{5,7},{6,8},{7,9},{8,10},{9,11},{10,... | collective-permute-start | bytes 1572872 | tf_op jit(solution)/shard_map/ppermute | solution.py:86
  8.7 20.4 %collective-permute-start.4 = (f32[256,512]{0,1:T(8,128)S(1)}, f32[256,512]{0,1:T(8,128)}, u32[]{:S(2)}, u32[]{:S(2)}) collective-permute-start(f32[256,512]{0,1:T(8,128)S(1)} %bitcast_select_fusion.1), channel_id=1, source_target_pairs={{0,14},{1,15},{2,0},{3,1},{4,2},{5,3},{6,4},{7,5},{8,6},{9,7},{10,... | collective-permute-start | bytes 1572872 | tf_op jit(solution)/shard_map/ppermute | solution.py:87
  17.3 60.9 %collective-permute-start.8 = (f32[256,512]{0,1:T(8,128)S(1)}, f32[256,512]{0,1:T(8,128)}, u32[]{:S(2)}, u32[]{:S(2)}) collective-permute-start(f32[256,512]{0,1:T(8,128)S(1)} %bitcast_select_fusion.1), channel_id=1, source_target_pairs={{0,1},{1,0},{2,3},{3,2},{4,5},{5,4},{6,7},{7,6},{8,9},{9,8},{10,11... | collective-permute-start | bytes 1572872 | tf_op jit(solution)/shard_map/ppermute | solution.py:94
  27.1 15.5 %collective-permute-start.1 = (f32[256,512]{0,1:T(8,128)}, f32[256,512]{0,1:T(8,128)S(1)}, u32[]{:S(2)}, u32[]{:S(2)}) collective-permute-start(f32[256,512]{0,1:T(8,128)} %collective-permute-done), channel_id=1, source_target_pairs={{0,2},{1,3},{2,4},{3,5},{4,6},{5,7},{6,8},{7,9},{8,10},{9,11},{10,... | collective-permute-start | bytes 1572872 | tf_op jit(solution)/shard_map/ppermute | solution.py:86
  29.1 15.5 %collective-permute-start.5 = (f32[256,512]{0,1:T(8,128)}, f32[256,512]{0,1:T(8,128)S(1)}, u32[]{:S(2)}, u32[]{:S(2)}) collective-permute-start(f32[256,512]{0,1:T(8,128)} %collective-permute-done.4), channel_id=1, source_target_pairs={{0,14},{1,15},{2,0},{3,1},{4,2},{5,3},{6,4},{7,5},{8,6},{9,7},{10,... | collective-permute-start | bytes 1572872 | tf_op jit(solution)/shard_map/ppermute | solution.py:87
  42.7 15.0 %collective-permute-start.2 = (f32[256,512]{0,1:T(8,128)S(1)}, f32[256,512]{0,1:T(8,128)S(1)}, u32[]{:S(2)}, u32[]{:S(2)}) collective-permute-start(f32[256,512]{0,1:T(8,128)S(1)} %collective-permute-done.1), channel_id=1, source_target_pairs={{0,2},{1,3},{2,4},{3,5},{4,6},{5,7},{6,8},{7,9},{8,10},{9,11},{10,... | collective-permute-start | bytes 1572872 | tf_op jit(solution)/shard_map/ppermute | solution.py:86
  44.6 15.8 %collective-permute-start.6 = (f32[256,512]{0,1:T(8,128)S(1)}, f32[256,512]{0,1:T(8,128)S(1)}, u32[]{:S(2)}, u32[]{:S(2)}) collective-permute-start(f32[256,512]{0,1:T(8,128)S(1)} %collective-permute-done.5), channel_id=1, source_target_pairs={{0,14},{1,15},{2,0},{3,1},{4,2},{5,3},{6,4},{7,5},{8,6},{9,7},{10,... | collective-permute-start | bytes 1572872 | tf_op jit(solution)/shard_map/ppermute | solution.py:87
  49.2 32.9 %collective-permute-start.9 = (f32[256,512]{0,1:T(8,128)}, f32[256,512]{0,1:T(8,128)S(1)}, u32[]{:S(2)}, u32[]{:S(2)}) collective-permute-start(f32[256,512]{0,1:T(8,128)} %collective-permute-done), channel_id=1, source_target_pairs={{0,1},{1,0},{2,3},{3,2},{4,5},{5,4},{6,7},{7,6},{8,9},{9,8},{10,11... | collective-permute-start | bytes 1572872 | tf_op jit(solution)/shard_map/ppermute | solution.py:94
  53.8 37.7 %collective-permute-start.15 = (f32[256,512]{0,1:T(8,128)}, f32[256,512]{0,1:T(8,128)S(1)}, u32[]{:S(2)}, u32[]{:S(2)}) collective-permute-start(f32[256,512]{0,1:T(8,128)} %collective-permute-done.4), channel_id=1, source_target_pairs={{0,1},{1,0},{2,3},{3,2},{4,5},{5,4},{6,7},{7,6},{8,9},{9,8},{10,11... | collective-permute-start | bytes 1572872 | tf_op jit(solution)/shard_map/ppermute | solution.py:94
  57.6 8.3 %collective-permute-start.3 = (f32[128,512]{0,1:T(8,128)S(1)}, f32[128,512]{0,1:T(8,128)S(1)}, u32[]{:S(2)}, u32[]{:S(2)}) collective-permute-start(f32[128,512]{0,1:T(8,128)S(1)} %slice.66), channel_id=1, source_target_pairs={{0,2},{1,3},{2,4},{3,5},{4,6},{5,7},{6,8},{7,9},{8,10},{9,11},{10,... | collective-permute-start | bytes 786440 | tf_op jit(solution)/shard_map/ppermute | solution.py:91
  60.4 11.1 %collective-permute-start.7 = (f32[128,512]{0,1:T(8,128)S(1)}, f32[128,512]{0,1:T(8,128)S(1)}, u32[]{:S(2)}, u32[]{:S(2)}) collective-permute-start(f32[128,512]{0,1:T(8,128)S(1)} %slice.67), channel_id=1, source_target_pairs={{0,14},{1,15},{2,0},{3,1},{4,2},{5,3},{6,4},{7,5},{8,6},{9,7},{10,... | collective-permute-start | bytes 786440 | tf_op jit(solution)/shard_map/ppermute | solution.py:92
  66.0 19.3 %collective-permute-start.10 = (f32[256,512]{0,1:T(8,128)S(1)}, f32[256,512]{0,1:T(8,128)S(1)}, u32[]{:S(2)}, u32[]{:S(2)}) collective-permute-start(f32[256,512]{0,1:T(8,128)S(1)} %collective-permute-done.1), channel_id=1, source_target_pairs={{0,1},{1,0},{2,3},{3,2},{4,5},{5,4},{6,7},{7,6},{8,9},{9,8},{10,11... | collective-permute-start | bytes 1572872 | tf_op jit(solution)/shard_map/ppermute | solution.py:94
  71.5 19.2 %collective-permute-start.14 = (f32[256,512]{0,1:T(8,128)S(1)}, f32[256,512]{0,1:T(8,128)S(1)}, u32[]{:S(2)}, u32[]{:S(2)}) collective-permute-start(f32[256,512]{0,1:T(8,128)S(1)} %collective-permute-done.5), channel_id=1, source_target_pairs={{0,1},{1,0},{2,3},{3,2},{4,5},{5,4},{6,7},{7,6},{8,9},{9,8},{10,11... | collective-permute-start | bytes 1572872 | tf_op jit(solution)/shard_map/ppermute | solution.py:94
  78.2 9.9 %collective-permute-start.11 = (f32[256,512]{0,1:T(8,128)S(1)}, f32[256,512]{0,1:T(8,128)S(1)}, u32[]{:S(2)}, u32[]{:S(2)}) collective-permute-start(f32[256,512]{0,1:T(8,128)S(1)} %collective-permute-done.2), channel_id=1, source_target_pairs={{0,1},{1,0},{2,3},{3,2},{4,5},{5,4},{6,7},{7,6},{8,9},{9,8},{10,11... | collective-permute-start | bytes 1572872 | tf_op jit(solution)/shard_map/ppermute | solution.py:94
  82.2 6.9 %collective-permute-start.12 = (f32[256,512]{0,1:T(8,128)S(1)}, f32[256,512]{0,1:T(8,128)S(1)}, u32[]{:S(2)}, u32[]{:S(2)}) collective-permute-start(f32[256,512]{0,1:T(8,128)S(1)} %constant_dynamic-update-slice_fusion), channel_id=1, source_target_pairs={{0,1},{1,0},{2,3},{3,2},{4,5},{5,4},{6,7},{7,6},{8,9},{9,8},{10,11... | collective-permute-start | bytes 1572872 | tf_op jit(solution)/shard_map/ppermute | solution.py:94
  85.3 4.6 %collective-permute-start.13 = (f32[256,512]{0,1:T(8,128)S(1)}, f32[256,512]{0,1:T(8,128)S(1)}, u32[]{:S(2)}, u32[]{:S(2)}) collective-permute-start(f32[256,512]{0,1:T(8,128)S(1)} %collective-permute-done.6), channel_id=1, source_target_pairs={{0,1},{1,0},{2,3},{3,2},{4,5},{5,4},{6,7},{7,6},{8,9},{9,8},{10,11... | collective-permute-start | bytes 1572872 | tf_op jit(solution)/shard_map/ppermute | solution.py:94
  184.1 5.6 %copy-start = (f32[6,256,512]{2,1,0:T(8,128)S(1)}, f32[6,256,512]{2,1,0:T(8,128)}, u32[]{:S(2)}) copy-start(f32[6,256,512]{2,1,0:T(8,128)} %copy.15) | copy-start | bytes 9437188
  184.1 8.4 %copy-start.1 = (f32[1,256,1536]{2,1,0:T(8,128)S(1)}, f32[1,256,1536]{2,1,0:T(8,128)}, u32[]{:S(2)}) copy-start(f32[1,256,1536]{2,1,0:T(8,128)} %get-tuple-element.12) | copy-start | bytes 4718596
  184.1 8.4 %copy-start.2 = (f32[1,256,1536]{2,1,0:T(8,128)S(1)}, f32[1,256,1536]{2,1,0:T(8,128)}, u32[]{:S(2)}) copy-start(f32[1,256,1536]{2,1,0:T(8,128)} %get-tuple-element.13) | copy-start | bytes 4718596
where the time goes:
time: 195 us; the launch traced here: 194 us
  Pallas kernels  59.1 us (30%)
  starting transfers between devices  56.4 us (29%)
  local copies, waits for them, and re-layouts  40.6 us (21%)
  matrix products  15.7 us (8%)
  waiting for transfers between devices  12.1 us (6%)
  other arithmetic  9.67 us (5%)
    pallas_call x1, Pallas kernels, spd_inverse(): pl.pallas_call(_gj_kernel, out_shape=jax.ShapeDtypeStruct((n, n), jnp.flo...  59.1 us
    ppermute x8, starting transfers between devices, ring_gather(): sib = [lax.ppermute(piece, AXES, swap) for piece in rel]  23.5 us
    ppermute x3, starting transfers between devices, ring_gather(): b = lax.ppermute(b, AXES, ccw)  17.7 us
    unnamed x25, local copies, waits for them, and re-layouts  14.9 us
    ppermute x3, waiting for transfers between devices, ring_gather(): a = lax.ppermute(a, AXES, cw)  11.9 us
    ppermute x3, starting transfers between devices, ring_gather(): a = lax.ppermute(a, AXES, cw)  8.64 us
    gather x1, local copies, waits for them, and re-layouts, ring_gather(): full = jnp.take(stacked, idx, axis=0)  7.69 us
    slice x2, local copies, waits for them, and re-layouts, body(): first_ext = g_a[:outer]  5.36 us
  transfers between devices with their start and end apart: 16, of which 3 were waited for; matrix products, arithmetic and copies ran while one was open for 10% of the time, Pallas kernels for 0%

commit v1 on v0

--- a/solution.py
+++ b/solution.py
@@ -76,31 +76,35 @@
     cw = ring_pairs(nbox, nrow, 1)
     ccw = ring_pairs(nbox, nrow, -1)
     swap = [(g, g ^ 1) for g in range(nbox * nrow)]
-    rows = mine.shape[0]
+    rows, cols = mine.shape
+    q = lax.axis_index("row") + nrow * (lax.axis_index("box") % 2)
+    z = q // 2
+    c = q % 2
     rel = [None] * chips
     rel[0] = mine
     a = mine
     b = mine
-    half = chips // 2
+    done_early = [0]
     for k in range(1, (chips - 1) // 2 + 1):
         a = lax.ppermute(a, AXES, cw)
         b = lax.ppermute(b, AXES, ccw)
         rel[k] = a
         rel[chips - k] = b
+        if k <= 2:
+            done_early += [k, chips - k]
     if chips % 2 == 0:
         top = lax.ppermute(a[: rows // 2], AXES, cw)
         bot = lax.ppermute(b[rows // 2 :], AXES, ccw)
-        rel[half] = jnp.concatenate([top, bot], 0)
-    sib = [lax.ppermute(piece, AXES, swap) for piece in rel]
-    stacked = jnp.stack(rel + sib)
-    q = lax.axis_index("row") + nrow * (lax.axis_index("box") % 2)
-    z = q // 2
-    c = q % 2
-    zs = jnp.arange(chips, dtype=jnp.int32)
-    offset = (z - zs) % chips
-    idx = jnp.stack([offset + chips * c, offset + chips * (1 - c)], 1).reshape(-1)
-    full = jnp.take(stacked, idx, axis=0)
-    return full.reshape(chips, 2 * rows, mine.shape[1])
+        rel[chips // 2] = jnp.concatenate([top, bot], 0)
+    done_late = [k for k in range(chips) if k not in done_early]
+    full = jnp.zeros((2 * chips, rows, cols), mine.dtype)
+    for group in (done_early, done_late):
+        sib = lax.ppermute(jnp.stack([rel[k] for k in group]), AXES, swap)
+        for i, k in enumerate(group):
+            slot = 2 * ((z - k) % chips)
+            full = lax.dynamic_update_index_in_dim(full, rel[k], slot + c, 0)
+            full = lax.dynamic_update_index_in_dim(full, sib[i], slot + 1 - c, 0)
+    return full.reshape(chips, 2 * rows, cols)
 
 
 def body(leaf_maps, iface_index):

time: 195 us -> 206 us (1.056)
  local copies, waits for them, and re-layouts: 40.6 us -> 59.8 us
  starting transfers between devices: 56.4 us -> 43.6 us
  waiting for transfers between devices: 12.1 us -> 21 us
  matrix products: 15.7 us -> 13.4 us
    dynamic_update_slice x0 -> x16, local copies, waits for them, and re-layouts: none -> 15.6 us  [the longest x8 7.89 us: ring_gather(): full = lax.dynamic_update_index_in_dim(full, rel[k], slot + c, 0)]
    ppermute x8 -> x2, starting transfers between devices: 23.5 us -> 10.7 us  [ring_gather(): sib = lax.ppermute(jnp.stack([rel[k] for k in group]), AXES, swap)]
    unnamed x25 -> x45, local copies, waits for them, and re-layouts: 14.9 us -> 2.62 us
    gather x1 -> x0, local copies, waits for them, and re-layouts: 7.69 us -> none  [ring_gather(): full = jnp.take(stacked, idx, axis=0)]
    another operation x2 -> x7, local copies, waits for them, and re-layouts: 0.97 us -> 7.89 us  [ring_gather(): sib = lax.ppermute(jnp.stack([rel[k] for k in group]), AXES, swap)]
    slice x2 -> x10, local copies, waits for them, and re-layouts: 3.91 us -> 10.6 us  [ring_gather(): full = lax.dynamic_update_index_in_dim(full, sib[i], slot + 1 - c, 0)]
    ppermute x3, waiting for transfers between devices: 11.9 us -> 17.4 us  [ring_gather(): a = lax.ppermute(a, AXES, cw)]
    broadcast_in_dim x0 -> x2, local copies, waits for them, and re-layouts: none -> 5.36 us  [the longest x1 4.37 us: ring_gather(): full = jnp.zeros((2 * chips, rows, cols), mine.dtype)]
  transfers between devices with their start and end apart: 16 -> 10, of which waited for: 3 -> 5; matrix products, arithmetic and copies ran while one was open for 10% -> 14% of each run, Pallas kernels for 0% -> 0%
where the time goes in v1:
time: 206 us; the launch traced here: 205 us
  local copies, waits for them, and re-layouts  59.8 us (29%)
  Pallas kernels  59.2 us (29%)
  starting transfers between devices  43.6 us (21%)
  waiting for transfers between devices  21 us (10%)
  matrix products  13.4 us (7%)
  other arithmetic  7.75 us (4%)
    pallas_call x1, Pallas kernels, spd_inverse(): pl.pallas_call(_gj_kernel, out_shape=jax.ShapeDtypeStruct((n, n), jnp.flo...  59.2 us
    ppermute x3, starting transfers between devices, ring_gather(): b = lax.ppermute(b, AXES, ccw)  17.7 us
    ppermute x3, waiting for transfers between devices, ring_gather(): a = lax.ppermute(a, AXES, cw)  17.4 us
    ppermute x2, starting transfers between devices, ring_gather(): sib = lax.ppermute(jnp.stack([rel[k] for k in group]), AXES, swap)  10.7 us
    slice x10, local copies, waits for them, and re-layouts, ring_gather(): full = lax.dynamic_update_index_in_dim(full, sib[i], slot + 1 - c, 0)  10.6 us
    ppermute x3, starting transfers between devices, ring_gather(): a = lax.ppermute(a, AXES, cw)  8.64 us
    dynamic_update_slice x8, local copies, waits for them, and re-layouts, ring_gather(): full = lax.dynamic_update_index_in_dim(full, rel[k], slot + c, 0)  7.89 us
    another operation x7, local copies, waits for them, and re-layouts, ring_gather(): sib = lax.ppermute(jnp.stack([rel[k] for k in group]), AXES, swap)  7.89 us
  transfers between devices with their start and end apart: 10, of which 5 were waited for; matrix products, arithmetic and copies ran while one was open for 14% of the time, Pallas kernels for 0%

profile of v1, /device:TPU:1, one launch (start us, length us, event | category | flops | bytes accessed | tf_op | source)
XLA Modules:
  0.0 205.4 jit_solution(5828590889615662398)
XLA Ops:
  0.7 1.1 slice.95
  2.0 1.6 gather_fusion
  3.8 4.8 %collective-permute-start = (f32[256,512]{0,1:T(8,128)S(1)}, f32[256,512]{0,1:T(8,128)S(1)}, u32[]{:S(2)}, u32[]{:S(2)}) collective-permute-start(f32[256,512]{0,1:T(8,128)S(1)} %bitcast_select_fusion.1), channel_id=1, source_target_pairs={{0,2},{1,3},{2,4},{3,5},{4,6},{5,7},{6,8},{7,9},{8,10},{9,11},{10,... | collective-permute-start | bytes 1572872 | tf_op jit(solution)/shard_map/ppermute | solution.py:89
  8.6 8.6 %collective-permute-start.1 = (f32[256,512]{0,1:T(8,128)S(1)}, f32[256,512]{0,1:T(8,128)S(1)}, u32[]{:S(2)}, u32[]{:S(2)}) collective-permute-start(f32[256,512]{0,1:T(8,128)S(1)} %bitcast_select_fusion.1), channel_id=1, source_target_pairs={{0,14},{1,15},{2,0},{3,1},{4,2},{5,3},{6,4},{7,5},{8,6},{9,7},{10,... | collective-permute-start | bytes 1572872 | tf_op jit(solution)/shard_map/ppermute | solution.py:90
  17.2 9.7 %collective-permute-done = f32[256,512]{0,1:T(8,128)S(1)} collective-permute-done((f32[256,512]{0,1:T(8,128)S(1)}, f32[256,512]{0,1:T(8,128)S(1)}, u32[]{:S(2)}, u32[]{:S(2)}) %collective-permute-start) | collective-permute-done | bytes 524320 | tf_op jit(solution)/shard_map/ppermute | solution.py:89
  26.9 1.9 collective-permute-start.2
  28.8 4.6 %collective-permute-start.3 = (f32[256,512]{0,1:T(8,128)S(1)}, f32[256,512]{0,1:T(8,128)S(1)}, u32[]{:S(2)}, u32[]{:S(2)}) collective-permute-start(f32[256,512]{0,1:T(8,128)S(1)} %collective-permute-done.1), channel_id=1, source_target_pairs={{0,14},{1,15},{2,0},{3,1},{4,2},{5,3},{6,4},{7,5},{8,6},{9,7},{10,... | collective-permute-start | bytes 1572872 | tf_op jit(solution)/shard_map/ppermute | solution.py:90
  33.4 1.1 constant_dynamic-update-slice_fusion.4
  34.5 0.8 constant_dynamic-update-slice_fusion.3
  35.3 0.8 constant_dynamic-update-slice_fusion.2
  36.2 6.0 %collective-permute-done.2 = f32[256,512]{0,1:T(8,128)S(1)} collective-permute-done((f32[256,512]{0,1:T(8,128)S(1)}, f32[256,512]{0,1:T(8,128)S(1)}, u32[]{:S(2)}, u32[]{:S(2)}) %collective-permute-start.2) | collective-permute-done | bytes 524320 | tf_op jit(solution)/shard_map/ppermute | solution.py:89
  42.2 1.9 collective-permute-start.5
  44.1 4.6 %collective-permute-start.7 = (f32[256,512]{0,1:T(8,128)S(1)}, f32[256,512]{0,1:T(8,128)S(1)}, u32[]{:S(2)}, u32[]{:S(2)}) collective-permute-start(f32[256,512]{0,1:T(8,128)S(1)} %collective-permute-done.3), channel_id=1, source_target_pairs={{0,14},{1,15},{2,0},{3,1},{4,2},{5,3},{6,4},{7,5},{8,6},{9,7},{10,... | collective-permute-start | bytes 1572872 | tf_op jit(solution)/shard_map/ppermute | solution.py:90
  48.7 0.9 constant_dynamic-update-slice_fusion.1
  49.6 0.8 constant_dynamic-update-slice_fusion
  50.4 4.6 %collective-permute-start.4 = (f32[5,256,512]{1,2,0:T(8,128)}, f32[5,256,512]{1,2,0:T(8,128)}, u32[]{:S(2)}, u32[]{:S(2)}) collective-permute-start(f32[5,256,512]{1,2,0:T(8,128)} %constant_dynamic-update-slice_fusion), channel_id=1, source_target_pairs={{0,1},{1,0},{2,3},{3,2},{4,5},{5,4},{6,7},{7,6},{8,9},{9,8},{10,11... | collective-permute-start | bytes 7864328 | tf_op jit(solution)/shard_map/ppermute | solution.py:102
  55.0 1.7 collective-permute-done.5
  56.7 1.9 collective-permute-start.6
  59.4 4.6 %collective-permute-start.8 = (f32[128,512]{0,1:T(8,128)}, f32[128,512]{0,1:T(8,128)}, u32[]{:S(2)}, u32[]{:S(2)}) collective-permute-start(f32[128,512]{0,1:T(8,128)} %slice.102), channel_id=1, source_target_pairs={{0,14},{1,15},{2,0},{3,1},{4,2},{5,3},{6,4},{7,5},{8,6},{9,7},{10,... | collective-permute-start | bytes 786440 | tf_op jit(solution)/shard_map/ppermute | solution.py:97
  64.0 1.2 collective-permute-done.6
  65.1 2.4 %collective-permute-done.8 = f32[128,512]{0,1:T(8,128)} collective-permute-done((f32[128,512]{0,1:T(8,128)}, f32[128,512]{0,1:T(8,128)}, u32[]{:S(2)}, u32[]{:S(2)}) %collective-permute-start.8) | collective-permute-done | bytes 262176 | tf_op jit(solution)/shard_map/ppermute | solution.py:97
  67.5 1.1 maximum_bitcast_fusion
  68.6 1.3 pad_maximum_fusion
  69.9 6.2 %collective-permute-start.9 = (f32[3,256,512]{1,2,0:T(8,128)}, f32[3,256,512]{1,2,0:T(8,128)}, u32[]{:S(2)}, u32[]{:S(2)}) collective-permute-start(f32[3,256,512]{1,2,0:T(8,128)} %pad_maximum_fusion), channel_id=1, source_target_pairs={{0,1},{1,0},{2,3},{3,2},{4,5},{5,4},{6,7},{7,6},{8,9},{9,8},{10,11... | collective-permute-start | bytes 4718600 | tf_op jit(solution)/shard_map/ppermute | solution.py:102
  76.3 2.0 copy.10
  79.2 4.4 %broadcast_in_dim.77 = f32[16,256,512]{2,1,0:T(8,128)} broadcast(f32[]{:T(128)} %constant.162.clone.1), dimensions={} | broadcast | bytes 8388612 | tf_op jit(solution)/shard_map/broadcast_in_dim | solution.py:100
  83.5 0.9 constant_dynamic-update-slice_fusion.20
  84.4 1.9 select_bitcast_fusion.1
  86.3 1.0 copy.12
  87.3 1.0 copy.14
  88.3 1.0 copy.16
  89.3 2.1 copy.18
  91.4 1.0 copy.20
  92.4 1.0 copy.24
  93.3 1.0 copy.22
  94.3 1.5 fusion.14
  95.8 1.0 copy.21
  96.8 1.0 copy.23
  98.0 2.0 fusion.13
  100.0 1.0 copy.11
  101.0 1.0 copy.13
  102.0 1.0 copy.15
  103.0 1.0 copy.17
  104.0 1.0 copy.19
  105.9 0.9 constant_dynamic-update-slice_fusion.18
  106.7 2.0 constant_dynamic-update-slice_fusion.17
  108.7 1.9 constant_dynamic-update-slice_fusion.16
  112.3 0.8 constant_dynamic-update-slice_fusion.13
  114.0 0.8 constant_dynamic-update-slice_fusion.11
  114.8 0.9 constant_dynamic-update-slice_fusion.10
  116.5 0.9 constant_dynamic-update-slice_fusion.8
  117.4 0.8 constant_dynamic-update-slice_fusion.7
  118.2 0.8 constant_dynamic-update-slice_fusion.6
  119.9 1.7 fusion.12
  121.6 6.3 %fusion.11 = (f32[6,256,512]{2,1,0:T(8,128)}, f32[6,256,512]{2,1,0:T(8,128)}) fusion(f32[16,256,512]{2,1,0:T(8,128)} %constant_dynamic-update-slice_fusion.5), kind=kLoop, calls=%fused_computation.61 | loop fusion | bytes 12582912 | tf_op jit(solution)/shard_map/slice | solution.py:132
  127.8 1.6 gather_fusion.1
  129.5 1.6 gather_fusion.2
  131.1 3.2 %fusion.10.a_ref = f32[512,512]{1,0:T(8,128)} fusion(f32[512,512]{1,0:T(8,128)S(1)} %gather_fusion.2, f32[512,512]{1,0:T(8,128)S(1)} %gather_fusion.1, pred[512]{0:T(512)(128)(4,1)S(1)} %get-tuple-element.28, pred[512]{0:T(512)(128)(4,1)S(1)} %get-tuple-element.29), kind=kOutput, calls=%fused_computation.60 | convolution fusion | flops 1611399168 | bytes 3146752 | tf_op jit(solution)/shard_map/dot_general | solution.py:130
  134.3 59.2 %shard_map.28 = f32[512,512]{1,0:T(8,128)} custom-call(f32[512,512]{1,0:T(8,128)} %fusion.10.a_ref), custom_call_target="tpu_custom_call" | custom-call | flops 1610612736 | bytes 2097152 | tf_op jit(solution)/shard_map/pallas_call | solution.py:53
  193.5 3.4 %fusion.9 = f32[512,512]{1,0:T(8,128)S(1)} fusion(f32[512,512]{1,0:T(8,128)} %shard_map.28, f32[512,512]{1,0:T(8,128)S(1)} %gather_fusion.2, f32[512,512]{1,0:T(8,128)S(1)} %gather_fusion.1, pred[512]{0:T(512)(128)(4,1)S(1)} %get-tuple-element.28, pred[512]{0:T(512)(128)(4,1)S(1)} %get-tuple-element.29), kind=kOutput, calls=%fused_computation.59 | convolution fusion | flops 1611399168 | bytes 4195328 | tf_op jit(solution)/shard_map/dot_general | solution.py:131
  196.9 1.2 fusion.1
  198.1 2.8 %convolution_bitcast_fusion.1 = f32[1,256,1536]{2,1,0:T(8,128)S(1)} fusion(f32[256,512]{1,0:T(8,128)S(1)} %fusion.1, f32[1536,512]{1,0:T(8,128)S(1)} %bitcast.46), kind=kOutput, calls=%fused_computation.6 | convolution fusion | flops 2415919104 | bytes 5242880 | tf_op jit(solution)/shard_map/dot_general | solution.py:145
  201.0 2.8 %convolution_bitcast_fusion = f32[1,256,1536]{2,1,0:T(8,128)S(1)} fusion(f32[256,512]{1,0:T(8,128)S(1)} %fusion.1, f32[1536,512]{1,0:T(8,128)S(1)} %bitcast.45), kind=kOutput, calls=%fused_computation.5 | convolution fusion | flops 2415919104 | bytes 5242880 | tf_op jit(solution)/shard_map/dot_general | solution.py:146
  203.9 1.5 fusion
  (68 shorter events, 7.9 us)
Async XLA Ops:
  3.8 4.8 %copy-start.5 = (f32[256,512]{0,1:T(8,128)}, f32[256,512]{0,1:T(8,128)S(1)}, u32[]{:S(2)}) copy-start(f32[256,512]{0,1:T(8,128)S(1)} %bitcast_select_fusion.1) | copy-start | bytes 1572868
  3.8 23.1 %collective-permute-start = (f32[256,512]{0,1:T(8,128)S(1)}, f32[256,512]{0,1:T(8,128)S(1)}, u32[]{:S(2)}, u32[]{:S(2)}) collective-permute-start(f32[256,512]{0,1:T(8,128)S(1)} %bitcast_select_fusion.1), channel_id=1, source_target_pairs={{0,2},{1,3},{2,4},{3,5},{4,6},{5,7},{6,8},{7,9},{8,10},{9,11},{10,... | collective-permute-start | bytes 1572872 | tf_op jit(solution)/shard_map/ppermute | solution.py:89
  8.6 20.2 %collective-permute-start.1 = (f32[256,512]{0,1:T(8,128)S(1)}, f32[256,512]{0,1:T(8,128)S(1)}, u32[]{:S(2)}, u32[]{:S(2)}) collective-permute-start(f32[256,512]{0,1:T(8,128)S(1)} %bitcast_select_fusion.1), channel_id=1, source_target_pairs={{0,14},{1,15},{2,0},{3,1},{4,2},{5,3},{6,4},{7,5},{8,6},{9,7},{10,... | collective-permute-start | bytes 1572872 | tf_op jit(solution)/shard_map/ppermute | solution.py:90
  26.9 15.3 %collective-permute-start.2 = (f32[256,512]{0,1:T(8,128)S(1)}, f32[256,512]{0,1:T(8,128)S(1)}, u32[]{:S(2)}, u32[]{:S(2)}) collective-permute-start(f32[256,512]{0,1:T(8,128)S(1)} %collective-permute-done), channel_id=1, source_target_pairs={{0,2},{1,3},{2,4},{3,5},{4,6},{5,7},{6,8},{7,9},{8,10},{9,11},{10,... | collective-permute-start | bytes 1572872 | tf_op jit(solution)/shard_map/ppermute | solution.py:89
  28.8 15.3 %collective-permute-start.3 = (f32[256,512]{0,1:T(8,128)S(1)}, f32[256,512]{0,1:T(8,128)S(1)}, u32[]{:S(2)}, u32[]{:S(2)}) collective-permute-start(f32[256,512]{0,1:T(8,128)S(1)} %collective-permute-done.1), channel_id=1, source_target_pairs={{0,14},{1,15},{2,0},{3,1},{4,2},{5,3},{6,4},{7,5},{8,6},{9,7},{10,... | collective-permute-start | bytes 1572872 | tf_op jit(solution)/shard_map/ppermute | solution.py:90
  42.2 14.5 %collective-permute-start.5 = (f32[256,512]{0,1:T(8,128)S(1)}, f32[256,512]{0,1:T(8,128)S(1)}, u32[]{:S(2)}, u32[]{:S(2)}) collective-permute-start(f32[256,512]{0,1:T(8,128)S(1)} %collective-permute-done.2), channel_id=1, source_target_pairs={{0,2},{1,3},{2,4},{3,5},{4,6},{5,7},{6,8},{7,9},{8,10},{9,11},{10,... | collective-permute-start | bytes 1572872 | tf_op jit(solution)/shard_map/ppermute | solution.py:89
  44.1 21.0 %copy-start.7 = (f32[256,512]{0,1:T(8,128)}, f32[256,512]{0,1:T(8,128)S(1)}, u32[]{:S(2)}) copy-start(f32[256,512]{0,1:T(8,128)S(1)} %collective-permute-done.3) | copy-start | bytes 1572868
  44.1 14.5 %collective-permute-start.7 = (f32[256,512]{0,1:T(8,128)S(1)}, f32[256,512]{0,1:T(8,128)S(1)}, u32[]{:S(2)}, u32[]{:S(2)}) collective-permute-start(f32[256,512]{0,1:T(8,128)S(1)} %collective-permute-done.3), channel_id=1, source_target_pairs={{0,14},{1,15},{2,0},{3,1},{4,2},{5,3},{6,4},{7,5},{8,6},{9,7},{10,... | collective-permute-start | bytes 1572872 | tf_op jit(solution)/shard_map/ppermute | solution.py:90
  50.4 47.6 %collective-permute-start.4 = (f32[5,256,512]{1,2,0:T(8,128)}, f32[5,256,512]{1,2,0:T(8,128)}, u32[]{:S(2)}, u32[]{:S(2)}) collective-permute-start(f32[5,256,512]{1,2,0:T(8,128)} %constant_dynamic-update-slice_fusion), channel_id=1, source_target_pairs={{0,1},{1,0},{2,3},{3,2},{4,5},{5,4},{6,7},{7,6},{8,9},{9,8},{10,11... | collective-permute-start | bytes 7864328 | tf_op jit(solution)/shard_map/ppermute | solution.py:102
  56.7 8.4 %collective-permute-start.6 = (f32[128,512]{0,1:T(8,128)S(1)}, f32[128,512]{0,1:T(8,128)}, u32[]{:S(2)}, u32[]{:S(2)}) collective-permute-start(f32[128,512]{0,1:T(8,128)S(1)} %slice.101), channel_id=1, source_target_pairs={{0,2},{1,3},{2,4},{3,5},{4,6},{5,7},{6,8},{7,9},{8,10},{9,11},{10,... | collective-permute-start | bytes 786440 | tf_op jit(solution)/shard_map/ppermute | solution.py:96
  59.4 8.2 %collective-permute-start.8 = (f32[128,512]{0,1:T(8,128)}, f32[128,512]{0,1:T(8,128)}, u32[]{:S(2)}, u32[]{:S(2)}) collective-permute-start(f32[128,512]{0,1:T(8,128)} %slice.102), channel_id=1, source_target_pairs={{0,14},{1,15},{2,0},{3,1},{4,2},{5,3},{6,4},{7,5},{8,6},{9,7},{10,... | collective-permute-start | bytes 786440 | tf_op jit(solution)/shard_map/ppermute | solution.py:97
  69.9 24.5 %collective-permute-start.9 = (f32[3,256,512]{1,2,0:T(8,128)}, f32[3,256,512]{1,2,0:T(8,128)}, u32[]{:S(2)}, u32[]{:S(2)}) collective-permute-start(f32[3,256,512]{1,2,0:T(8,128)} %pad_maximum_fusion), channel_id=1, source_target_pairs={{0,1},{1,0},{2,3},{3,2},{4,5},{5,4},{6,7},{7,6},{8,9},{9,8},{10,11... | collective-permute-start | bytes 4718600 | tf_op jit(solution)/shard_map/ppermute | solution.py:102
  79.2 4.4 %copy-start.9 = (f32[1,256,512]{2,1,0:T(8,128)S(1)}, f32[1,256,512]{2,1,0:T(8,128)}, u32[]{:S(2)}) copy-start(f32[1,256,512]{2,1,0:T(8,128)} %copy.10) | copy-start | bytes 1572868
  79.2 5.3 %copy-start.4 = (f32[1,256,2048]{2,1,0:T(8,128)S(1)}, f32[1,256,2048]{2,1,0:T(8,128)}, u32[]{:S(2)}) copy-start(f32[1,256,2048]{2,1,0:T(8,128)} %param.4) | copy-start | bytes 6291460
  101.0 4.0 %copy-start.20 = (f32[1,256,512]{2,1,0:T(8,128)S(1)}, f32[1,256,512]{2,1,0:T(8,128)}, u32[]{:S(2)}) copy-start(f32[1,256,512]{2,1,0:T(8,128)} %copy.11) | copy-start | bytes 1572868
  103.0 2.8 %copy-start.16 = (f32[1,256,512]{2,1,0:T(8,128)S(1)}, f32[1,256,512]{2,1,0:T(8,128)}, u32[]{:S(2)}) copy-start(f32[1,256,512]{2,1,0:T(8,128)} %copy.12) | copy-start | bytes 1572868
  104.0 6.7 %copy-start.19 = (f32[1,256,512]{2,1,0:T(8,128)S(1)}, f32[1,256,512]{2,1,0:T(8,128)}, u32[]{:S(2)}) copy-start(f32[1,256,512]{2,1,0:T(8,128)} %copy.15) | copy-start | bytes 1572868
  104.0 7.5 %copy-start.15 = (f32[1,256,512]{2,1,0:T(8,128)S(1)}, f32[1,256,512]{2,1,0:T(8,128)}, u32[]{:S(2)}) copy-start(f32[1,256,512]{2,1,0:T(8,128)} %copy.16) | copy-start | bytes 1572868
  105.0 7.3 %copy-start.18 = (f32[1,256,512]{2,1,0:T(8,128)S(1)}, f32[1,256,512]{2,1,0:T(8,128)}, u32[]{:S(2)}) copy-start(f32[1,256,512]{2,1,0:T(8,128)} %copy.17) | copy-start | bytes 1572868
  105.9 7.3 %copy-start.13 = (f32[1,256,512]{2,1,0:T(8,128)S(1)}, f32[1,256,512]{2,1,0:T(8,128)}, u32[]{:S(2)}) copy-start(f32[1,256,512]{2,1,0:T(8,128)} %copy.18) | copy-start | bytes 1572868
  106.7 7.2 %copy-start.17 = (f32[1,256,512]{2,1,0:T(8,128)S(1)}, f32[1,256,512]{2,1,0:T(8,128)}, u32[]{:S(2)}) copy-start(f32[1,256,512]{2,1,0:T(8,128)} %copy.19) | copy-start | bytes 1572868
  108.7 6.1 %copy-start.11 = (f32[1,256,512]{2,1,0:T(8,128)S(1)}, f32[1,256,512]{2,1,0:T(8,128)}, u32[]{:S(2)}) copy-start(f32[1,256,512]{2,1,0:T(8,128)} %copy.20) | copy-start | bytes 1572868
  110.7 5.0 %copy-start.14 = (f32[1,256,512]{2,1,0:T(8,128)S(1)}, f32[1,256,512]{2,1,0:T(8,128)}, u32[]{:S(2)}) copy-start(f32[1,256,512]{2,1,0:T(8,128)} %copy.21) | copy-start | bytes 1572868
  111.5 5.0 %copy-start.10 = (f32[1,256,512]{2,1,0:T(8,128)S(1)}, f32[1,256,512]{2,1,0:T(8,128)}, u32[]{:S(2)}) copy-start(f32[1,256,512]{2,1,0:T(8,128)} %copy.22) | copy-start | bytes 1572868
  112.3 5.1 %copy-start.12 = (f32[1,256,512]{2,1,0:T(8,128)S(1)}, f32[1,256,512]{2,1,0:T(8,128)}, u32[]{:S(2)}) copy-start(f32[1,256,512]{2,1,0:T(8,128)} %copy.23) | copy-start | bytes 1572868
  113.2 5.0 %copy-start.8 = (f32[1,256,512]{2,1,0:T(8,128)S(1)}, f32[1,256,512]{2,1,0:T(8,128)}, u32[]{:S(2)}) copy-start(f32[1,256,512]{2,1,0:T(8,128)} %copy.24) | copy-start | bytes 1572868
  193.5 3.4 %copy-start.6 = (f32[256,512]{0,1:T(8,128)S(1)}, f32[256,512]{0,1:T(8,128)}, u32[]{:S(2)}) copy-start(f32[256,512]{0,1:T(8,128)} %copy-done.5) | copy-start | bytes 1572868
  193.5 4.6 %copy-start.1 = (f32[6,256,512]{2,1,0:T(8,128)S(1)}, f32[6,256,512]{2,1,0:T(8,128)}, u32[]{:S(2)}) copy-start(f32[6,256,512]{2,1,0:T(8,128)} %get-tuple-element.10) | copy-start | bytes 9437188
  198.1 2.9 %copy-start = (f32[6,256,512]{2,1,0:T(8,128)S(1)}, f32[6,256,512]{2,1,0:T(8,128)}, u32[]{:S(2)}) copy-start(f32[6,256,512]{2,1,0:T(8,128)} %get-tuple-element.11) | copy-start | bytes 9437188
  201.0 2.9 %copy-start.2 = (f32[1,256,1536]{2,1,0:T(8,128)S(1)}, f32[1,256,1536]{2,1,0:T(8,128)}, u32[]{:S(2)}) copy-start(f32[1,256,1536]{2,1,0:T(8,128)} %get-tuple-element.19) | copy-start | bytes 4718596
  201.0 2.9 %copy-start.3 = (f32[1,256,1536]{2,1,0:T(8,128)S(1)}, f32[1,256,1536]{2,1,0:T(8,128)}, u32[]{:S(2)}) copy-start(f32[1,256,1536]{2,1,0:T(8,128)} %get-tuple-element.20) | copy-start | bytes 4718596

commit v2 on v0

--- a/solution.py
+++ b/solution.py
@@ -9,30 +9,49 @@
 HI = lax.Precision.HIGHEST
 
 
-def _gj_kernel(a_ref, o_ref, p_ref):
+def _panel_inverse(p_ref, s_ref):
+    nb = p_ref.shape[0]
+    ns = s_ref.shape[0]
+    lane_s = lax.broadcasted_iota(jnp.int32, (ns, nb), 1)
+    lane_r = lax.broadcasted_iota(jnp.int32, (1, nb), 1)
+    sub_c = lax.broadcasted_iota(jnp.int32, (ns, 1), 0)
+    sub_p = lax.broadcasted_iota(jnp.int32, (nb, nb), 0)
+    lane_p = lax.broadcasted_iota(jnp.int32, (nb, nb), 1)
+    for kb in range(nb // ns):
+        lo = kb * ns
+        s_ref[...] = p_ref[lo:lo + ns, :]
+
+        def step(j, carry):
+            pc = lo + j
+            slab = s_ref[...]
+            row = s_ref[pl.ds(j, 1), :]
+            piv = jnp.sum(jnp.where(lane_r == pc, row, 0.0), axis=1, keepdims=True)
+            rnew = jnp.where(lane_r == pc, 1.0, row) / piv
+            col = jnp.sum(jnp.where(lane_s == pc, slab, 0.0), axis=1, keepdims=True)
+            col = jnp.where(sub_c == j, 0.0, col)
+            s_ref[...] = jnp.where(lane_s == pc, 0.0, slab) - col * rnew
+            s_ref[pl.ds(j, 1), :] = rnew
+            return carry
+
+        lax.fori_loop(0, ns, step, 0)
+        whole = p_ref[...]
+        in_rows = jnp.logical_and(sub_p >= lo, sub_p < lo + ns)
+        in_cols = jnp.logical_and(lane_p >= lo, lane_p < lo + ns)
+        cols = jnp.where(jnp.logical_and(in_cols, jnp.logical_not(in_rows)), whole, 0.0)
+        p_ref[lo:lo + ns, :] = s_ref[...]
+        e = jnp.where(in_rows, p_ref[...], 0.0)
+        upd = jnp.where(in_cols, 0.0, whole) - jnp.dot(cols, e, precision=HI, preferred_element_type=jnp.float32)
+        p_ref[...] = jnp.where(in_rows, e, upd)
+
+
+def _gj_kernel(a_ref, o_ref, p_ref, s_ref):
     n = a_ref.shape[0]
     nb = p_ref.shape[0]
     o_ref[...] = a_ref[...]
-    lane_p = lax.broadcasted_iota(jnp.int32, (nb, nb), 1)
-    lane_r = lax.broadcasted_iota(jnp.int32, (1, nb), 1)
-    sub_c = lax.broadcasted_iota(jnp.int32, (nb, 1), 0)
     for kb in range(n // nb):
         lo = kb * nb
         p_ref[...] = o_ref[lo:lo + nb, lo:lo + nb]
-
-        def step(j, carry):
-            block = p_ref[...]
-            row = p_ref[pl.ds(j, 1), :]
-            piv = jnp.sum(jnp.where(lane_r == j, row, 0.0), axis=1, keepdims=True)
-            inv = 1.0 / piv
-            rnew = jnp.where(lane_r == j, 1.0, row) * inv
-            col = jnp.sum(jnp.where(lane_p == j, block, 0.0), axis=1, keepdims=True)
-            col = jnp.where(sub_c == j, 0.0, col)
-            p_ref[...] = jnp.where(lane_p == j, 0.0, block) - col * rnew
-            p_ref[pl.ds(j, 1), :] = rnew
-            return carry
-
-        lax.fori_loop(0, nb, step, 0)
+        _panel_inverse(p_ref, s_ref)
         pinv = p_ref[...]
         lane_n = lax.broadcasted_iota(jnp.int32, (nb, n), 1)
         sub_n = lax.broadcasted_iota(jnp.int32, (nb, n), 0)
@@ -55,7 +74,7 @@
         out_shape=jax.ShapeDtypeStruct((n, n), jnp.float32),
         in_specs=[pl.BlockSpec(memory_space=pltpu.VMEM)],
         out_specs=pl.BlockSpec(memory_space=pltpu.VMEM),
-        scratch_shapes=[pltpu.VMEM((nb, nb), jnp.float32)],
+        scratch_shapes=[pltpu.VMEM((nb, nb), jnp.float32), pltpu.VMEM((32, nb), jnp.float32)],
         cost_estimate=pl.CostEstimate(flops=2 * n * n * n * 6, bytes_accessed=8 * n * n, transcendentals=0),
     )(a)
 

time: 195 us -> 195 us (level)
  no operation moved by 1% of the time
where the time goes in v2:
time: 195 us; the launch traced here: 194 us
  Pallas kernels  59.1 us (30%)
  starting transfers between devices  56.4 us (29%)
  local copies, waits for them, and re-layouts  40.6 us (21%)
  matrix products  15.7 us (8%)
  waiting for transfers between devices  12.1 us (6%)
  other arithmetic  9.67 us (5%)
    pallas_call x1, Pallas kernels, spd_inverse(): pl.pallas_call(_gj_kernel, out_shape=jax.ShapeDtypeStruct((n, n), jnp.flo...  59.1 us
    ppermute x8, starting transfers between devices, ring_gather(): sib = [lax.ppermute(piece, AXES, swap) for piece in rel]  23.5 us
    ppermute x3, starting transfers between devices, ring_gather(): b = lax.ppermute(b, AXES, ccw)  17.7 us
    unnamed x25, local copies, waits for them, and re-layouts  14.9 us
    ppermute x3, waiting for transfers between devices, ring_gather(): a = lax.ppermute(a, AXES, cw)  11.9 us
    ppermute x3, starting transfers between devices, ring_gather(): a = lax.ppermute(a, AXES, cw)  8.64 us
    gather x1, local copies, waits for them, and re-layouts, ring_gather(): full = jnp.take(stacked, idx, axis=0)  7.69 us
    slice x2, local copies, waits for them, and re-layouts, body(): first_ext = g_a[:outer]  5.36 us
  transfers between devices with their start and end apart: 16, of which 3 were waited for; matrix products, arithmetic and copies ran while one was open for 10% of the time, Pallas kernels for 0%

profile of v2, /device:TPU:1, one launch (start us, length us, event | category | flops | bytes accessed | tf_op | source)
XLA Modules:
  0.0 194.0 jit_solution(4325595877531704749)
XLA Ops:
  0.0 0.9 compare_select_fusion
  0.9 1.1 slice.65
  2.0 0.2 copy.9
  2.2 1.6 gather_fusion
  3.8 0.1 bitcast_select_fusion.1
  3.9 4.8 %collective-permute-start = (f32[256,512]{0,1:T(8,128)S(1)}, f32[256,512]{0,1:T(8,128)}, u32[]{:S(2)}, u32[]{:S(2)}) collective-permute-start(f32[256,512]{0,1:T(8,128)S(1)} %bitcast_select_fusion.1), channel_id=1, source_target_pairs={{0,2},{1,3},{2,4},{3,5},{4,6},{5,7},{6,8},{7,9},{8,10},{9,11},{10,... | collective-permute-start | bytes 1572872 | tf_op jit(solution)/shard_map/ppermute | solution.py:105
  8.7 8.6 %collective-permute-start.4 = (f32[256,512]{0,1:T(8,128)S(1)}, f32[256,512]{0,1:T(8,128)}, u32[]{:S(2)}, u32[]{:S(2)}) collective-permute-start(f32[256,512]{0,1:T(8,128)S(1)} %bitcast_select_fusion.1), channel_id=1, source_target_pairs={{0,14},{1,15},{2,0},{3,1},{4,2},{5,3},{6,4},{7,5},{8,6},{9,7},{10,... | collective-permute-start | bytes 1572872 | tf_op jit(solution)/shard_map/ppermute | solution.py:106
  17.3 2.9 %collective-permute-start.8 = (f32[256,512]{0,1:T(8,128)S(1)}, f32[256,512]{0,1:T(8,128)}, u32[]{:S(2)}, u32[]{:S(2)}) collective-permute-start(f32[256,512]{0,1:T(8,128)S(1)} %bitcast_select_fusion.1), channel_id=1, source_target_pairs={{0,1},{1,0},{2,3},{3,2},{4,5},{5,4},{6,7},{7,6},{8,9},{9,8},{10,11... | collective-permute-start | bytes 1572872 | tf_op jit(solution)/shard_map/ppermute | solution.py:113
  20.3 0.8 constant_dynamic-slice_fusion.1
  21.1 1.9 select_bitcast_fusion.1
  23.0 0.1 copy.10
  23.1 0.1 reshape.235
  23.2 3.9 %collective-permute-done = f32[256,512]{0,1:T(8,128)} collective-permute-done((f32[256,512]{0,1:T(8,128)S(1)}, f32[256,512]{0,1:T(8,128)}, u32[]{:S(2)}, u32[]{:S(2)}) %collective-permute-start) | collective-permute-done | bytes 524320 | tf_op jit(solution)/shard_map/ppermute | solution.py:105
  27.1 1.9 collective-permute-start.1
  29.1 0.1 reshape.234
  29.1 0.0 collective-permute-done.4
  29.1 4.6 %collective-permute-start.5 = (f32[256,512]{0,1:T(8,128)}, f32[256,512]{0,1:T(8,128)S(1)}, u32[]{:S(2)}, u32[]{:S(2)}) collective-permute-start(f32[256,512]{0,1:T(8,128)} %collective-permute-done.4), channel_id=1, source_target_pairs={{0,14},{1,15},{2,0},{3,1},{4,2},{5,3},{6,4},{7,5},{8,6},{9,7},{10,... | collective-permute-start | bytes 1572872 | tf_op jit(solution)/shard_map/ppermute | solution.py:106
  33.7 0.9 fusion.1
  34.7 8.0 %collective-permute-done.1 = f32[256,512]{0,1:T(8,128)S(1)} collective-permute-done((f32[256,512]{0,1:T(8,128)}, f32[256,512]{0,1:T(8,128)S(1)}, u32[]{:S(2)}, u32[]{:S(2)}) %collective-permute-start.1) | collective-permute-done | bytes 524320 | tf_op jit(solution)/shard_map/ppermute | solution.py:105
  42.7 1.9 collective-permute-start.2
  44.6 0.0 collective-permute-done.5
  44.6 4.6 %collective-permute-start.6 = (f32[256,512]{0,1:T(8,128)S(1)}, f32[256,512]{0,1:T(8,128)S(1)}, u32[]{:S(2)}, u32[]{:S(2)}) collective-permute-start(f32[256,512]{0,1:T(8,128)S(1)} %collective-permute-done.5), channel_id=1, source_target_pairs={{0,14},{1,15},{2,0},{3,1},{4,2},{5,3},{6,4},{7,5},{8,6},{9,7},{10,... | collective-permute-start | bytes 1572872 | tf_op jit(solution)/shard_map/ppermute | solution.py:106
  49.2 4.6 %collective-permute-start.9 = (f32[256,512]{0,1:T(8,128)}, f32[256,512]{0,1:T(8,128)S(1)}, u32[]{:S(2)}, u32[]{:S(2)}) collective-permute-start(f32[256,512]{0,1:T(8,128)} %collective-permute-done), channel_id=1, source_target_pairs={{0,1},{1,0},{2,3},{3,2},{4,5},{5,4},{6,7},{7,6},{8,9},{9,8},{10,11... | collective-permute-start | bytes 1572872 | tf_op jit(solution)/shard_map/ppermute | solution.py:113
  53.8 1.9 collective-permute-start.15
  55.7 1.9 bitcast_dynamic-update-slice_fusion.14
  57.6 1.9 collective-permute-start.3
  59.6 0.8 bitcast_dynamic-update-slice_fusion.13
  60.4 4.6 %collective-permute-start.7 = (f32[128,512]{0,1:T(8,128)S(1)}, f32[128,512]{0,1:T(8,128)S(1)}, u32[]{:S(2)}, u32[]{:S(2)}) collective-permute-start(f32[128,512]{0,1:T(8,128)S(1)} %slice.67), channel_id=1, source_target_pairs={{0,14},{1,15},{2,0},{3,1},{4,2},{5,3},{6,4},{7,5},{8,6},{9,7},{10,... | collective-permute-start | bytes 786440 | tf_op jit(solution)/shard_map/ppermute | solution.py:111
  65.0 0.8 bitcast_dynamic-update-slice_fusion.12
  65.8 0.1 collective-permute-done.3
  66.0 5.5 %collective-permute-start.10 = (f32[256,512]{0,1:T(8,128)S(1)}, f32[256,512]{0,1:T(8,128)S(1)}, u32[]{:S(2)}, u32[]{:S(2)}) collective-permute-start(f32[256,512]{0,1:T(8,128)S(1)} %collective-permute-done.1), channel_id=1, source_target_pairs={{0,1},{1,0},{2,3},{3,2},{4,5},{5,4},{6,7},{7,6},{8,9},{9,8},{10,11... | collective-permute-start | bytes 1572872 | tf_op jit(solution)/shard_map/ppermute | solution.py:113
  71.5 2.3 %collective-permute-start.14 = (f32[256,512]{0,1:T(8,128)S(1)}, f32[256,512]{0,1:T(8,128)S(1)}, u32[]{:S(2)}, u32[]{:S(2)}) collective-permute-start(f32[256,512]{0,1:T(8,128)S(1)} %collective-permute-done.5), channel_id=1, source_target_pairs={{0,1},{1,0},{2,3},{3,2},{4,5},{5,4},{6,7},{7,6},{8,9},{9,8},{10,11... | collective-permute-start | bytes 1572872 | tf_op jit(solution)/shard_map/ppermute | solution.py:113
  73.9 0.8 bitcast_dynamic-update-slice_fusion.11
  74.7 0.8 bitcast_dynamic-update-slice_fusion.10
  75.5 0.8 bitcast_dynamic-update-slice_fusion.9
  76.4 1.9 bitcast_dynamic-update-slice_fusion.8
  78.2 2.0 %collective-permute-start.11 = (f32[256,512]{0,1:T(8,128)S(1)}, f32[256,512]{0,1:T(8,128)S(1)}, u32[]{:S(2)}, u32[]{:S(2)}) collective-permute-start(f32[256,512]{0,1:T(8,128)S(1)} %collective-permute-done.2), channel_id=1, source_target_pairs={{0,1},{1,0},{2,3},{3,2},{4,5},{5,4},{6,7},{7,6},{8,9},{9,8},{10,11... | collective-permute-start | bytes 1572872 | tf_op jit(solution)/shard_map/ppermute | solution.py:113
  80.3 1.9 bitcast_dynamic-update-slice_fusion.7
  82.2 2.3 %collective-permute-start.12 = (f32[256,512]{0,1:T(8,128)S(1)}, f32[256,512]{0,1:T(8,128)S(1)}, u32[]{:S(2)}, u32[]{:S(2)}) collective-permute-start(f32[256,512]{0,1:T(8,128)S(1)} %constant_dynamic-update-slice_fusion), channel_id=1, source_target_pairs={{0,1},{1,0},{2,3},{3,2},{4,5},{5,4},{6,7},{7,6},{8,9},{9,8},{10,11... | collective-permute-start | bytes 1572872 | tf_op jit(solution)/shard_map/ppermute | solution.py:113
  84.4 0.8 bitcast_dynamic-update-slice_fusion.6
  85.3 2.0 %collective-permute-start.13 = (f32[256,512]{0,1:T(8,128)S(1)}, f32[256,512]{0,1:T(8,128)S(1)}, u32[]{:S(2)}, u32[]{:S(2)}) collective-permute-start(f32[256,512]{0,1:T(8,128)S(1)} %collective-permute-done.6), channel_id=1, source_target_pairs={{0,1},{1,0},{2,3},{3,2},{4,5},{5,4},{6,7},{7,6},{8,9},{9,8},{10,11... | collective-permute-start | bytes 1572872 | tf_op jit(solution)/shard_map/ppermute | solution.py:113
  87.3 0.8 bitcast_dynamic-update-slice_fusion.5
  88.2 0.8 bitcast_dynamic-update-slice_fusion.4
  89.0 0.8 bitcast_dynamic-update-slice_fusion.3
  89.9 0.8 bitcast_dynamic-update-slice_fusion.2
  90.7 0.8 bitcast_dynamic-update-slice_fusion.1
  91.5 0.9 bitcast_dynamic-update-slice_fusion
  92.4 7.7 %gather_fusion.1 = f32[16,256,512]{1,2,0:T(8,128)} fusion(f32[16,256,512]{1,2,0:T(8,128)} %bitcast_dynamic-update-slice_fusion, s32[1024]{0:T(1024)S(1)} %pad_clamp_fusion.2), kind=kCustom, calls=%fused_computation.3 | custom fusion | bytes 16777280 | tf_op jit(solution)/shard_map/jit(_take)/gather | solution.py:121
  100.1 4.2 %broadcast_select_fusion = f32[16,256,512]{1,2,0:T(8,128)S(1)} fusion(f32[16,256,512]{1,2,0:T(8,128)} %gather_fusion.1, pred[16]{0:T(512)(128)(4,1)S(1)} %compare_and_fusion.2), kind=kLoop, calls=%fused_computation.4 | loop fusion | flops 2097152 | bytes 16777232 | tf_op jit(solution)/shard_map/jit(_take)/select_n | solution.py:121
  104.4 0.1 fusion.15
  104.5 3.0 %fusion.14 = (f32[6,256,512]{1,2,0:T(8,128)}, f32[6,256,512]{1,2,0:T(8,128)}) fusion(f32[16,256,512]{1,2,0:T(8,128)S(1)} %broadcast_select_fusion), kind=kLoop, calls=%fused_computation.70 | loop fusion | bytes 12582912 | tf_op jit(solution)/shard_map/slice | solution.py:147
  107.5 0.3 copy.12
  107.8 0.3 copy.13
  108.2 1.8 gather_fusion.2
  110.0 1.6 gather_fusion.3
  111.6 3.1 %fusion.13.a_ref = f32[512,512]{1,0:T(8,128)} fusion(f32[512,512]{1,0:T(8,128)S(1)} %gather_fusion.3, f32[512,512]{1,0:T(8,128)S(1)} %gather_fusion.2, pred[512]{0:T(512)(128)(4,1)S(1)} %get-tuple-element.22, pred[512]{0:T(512)(128)(4,1)S(1)} %get-tuple-element.23), kind=kOutput, calls=%fused_computation.69 | convolution fusion | flops 1611399168 | bytes 3146752 | tf_op jit(solution)/shard_map/dot_general | solution.py:145
  114.7 59.1 %shard_map.28 = f32[512,512]{1,0:T(8,128)} custom-call(f32[512,512]{1,0:T(8,128)} %fusion.13.a_ref), custom_call_target="tpu_custom_call" | custom-call | flops 1610612736 | bytes 2097152 | tf_op jit(solution)/shard_map/pallas_call | solution.py:72
  173.9 4.2 %fusion.12 = f32[512,512]{1,0:T(8,128)} fusion(f32[512,512]{1,0:T(8,128)} %shard_map.28, f32[512,512]{1,0:T(8,128)S(1)} %gather_fusion.3, f32[512,512]{1,0:T(8,128)S(1)} %gather_fusion.2, pred[512]{0:T(512)(128)(4,1)S(1)} %get-tuple-element.22, pred[512]{0:T(512)(128)(4,1)S(1)} %get-tuple-element.23), kind=kOutput, calls=%fused_computation.68 | convolution fusion | flops 1611399168 | bytes 4195328 | tf_op jit(solution)/shard_map/dot_general | solution.py:146
  178.1 2.4 %copy.14 = f32[6,256,512]{2,1,0:T(8,128)S(1)} copy(f32[6,256,512]{1,2,0:T(8,128)} %get-tuple-element.8) | data formatting | bytes 6291456 | tf_op jit(solution)/shard_map/slice | solution.py:147
  180.5 3.6 %copy.15 = f32[6,256,512]{2,1,0:T(8,128)} copy(f32[6,256,512]{1,2,0:T(8,128)} %get-tuple-element.9) | data formatting | bytes 6291456 | tf_op jit(solution)/shard_map/slice | solution.py:148
  184.1 2.7 %fusion.2 = f32[256,512]{1,0:T(8,128)S(1)} fusion(f32[512,512]{1,0:T(8,128)} %fusion.12, f32[256,512]{0,1:T(8,128)} %copy-done.4, s32[256]{0:T(256)S(1)} %fusion.9, s32[512]{0:T(512)S(1)} %bitcast.71, pred[256]{0:T(512)(128)(4,1)S(1)} %get-tuple-element.20), kind=kOutput, calls=%fused_computation.30 | convolution fusion | flops 805699584 | bytes 2100480 | tf_op jit(solution)/shard_map/dot_general | solution.py:158
  186.7 2.8 %convolution_bitcast_fusion.1 = f32[1,256,1536]{2,1,0:T(8,128)S(1)} fusion(f32[256,512]{1,0:T(8,128)S(1)} %fusion.2, f32[1536,512]{1,0:T(8,128)S(1)} %bitcast.66), kind=kOutput, calls=%fused_computation.8 | convolution fusion | flops 2415919104 | bytes 5242880 | tf_op jit(solution)/shard_map/dot_general | solution.py:160
  189.6 2.8 %convolution_bitcast_fusion = f32[1,256,1536]{2,1,0:T(8,128)S(1)} fusion(f32[256,512]{1,0:T(8,128)S(1)} %fusion.2, f32[1536,512]{1,0:T(8,128)S(1)} %bitcast.67), kind=kOutput, calls=%fused_computation.7 | convolution fusion | flops 2415919104 | bytes 5242880 | tf_op jit(solution)/shard_map/dot_general | solution.py:161
  192.5 1.5 fusion
  (38 shorter events, 0.2 us)
Async XLA Ops:
  0.0 21.1 %copy-start.3 = (f32[1,256,2048]{2,1,0:T(8,128)S(1)}, f32[1,256,2048]{2,1,0:T(8,128)}, u32[]{:S(2)}) copy-start(f32[1,256,2048]{2,1,0:T(8,128)} %param.4) | copy-start | bytes 6291460
  3.9 81.4 %copy-start.4 = (f32[256,512]{0,1:T(8,128)}, f32[256,512]{0,1:T(8,128)S(1)}, u32[]{:S(2)}) copy-start(f32[256,512]{0,1:T(8,128)S(1)} %bitcast_select_fusion.1) | copy-start | bytes 1572868
  3.9 23.2 %collective-permute-start = (f32[256,512]{0,1:T(8,128)S(1)}, f32[256,512]{0,1:T(8,128)}, u32[]{:S(2)}, u32[]{:S(2)}) collective-permute-start(f32[256,512]{0,1:T(8,128)S(1)} %bitcast_select_fusion.1), channel_id=1, source_target_pairs={{0,2},{1,3},{2,4},{3,5},{4,6},{5,7},{6,8},{7,9},{8,10},{9,11},{10,... | collective-permute-start | bytes 1572872 | tf_op jit(solution)/shard_map/ppermute | solution.py:105
  8.7 20.4 %collective-permute-start.4 = (f32[256,512]{0,1:T(8,128)S(1)}, f32[256,512]{0,1:T(8,128)}, u32[]{:S(2)}, u32[]{:S(2)}) collective-permute-start(f32[256,512]{0,1:T(8,128)S(1)} %bitcast_select_fusion.1), channel_id=1, source_target_pairs={{0,14},{1,15},{2,0},{3,1},{4,2},{5,3},{6,4},{7,5},{8,6},{9,7},{10,... | collective-permute-start | bytes 1572872 | tf_op jit(solution)/shard_map/ppermute | solution.py:106
  17.3 60.9 %collective-permute-start.8 = (f32[256,512]{0,1:T(8,128)S(1)}, f32[256,512]{0,1:T(8,128)}, u32[]{:S(2)}, u32[]{:S(2)}) collective-permute-start(f32[256,512]{0,1:T(8,128)S(1)} %bitcast_select_fusion.1), channel_id=1, source_target_pairs={{0,1},{1,0},{2,3},{3,2},{4,5},{5,4},{6,7},{7,6},{8,9},{9,8},{10,11... | collective-permute-start | bytes 1572872 | tf_op jit(solution)/shard_map/ppermute | solution.py:113
  27.1 15.5 %collective-permute-start.1 = (f32[256,512]{0,1:T(8,128)}, f32[256,512]{0,1:T(8,128)S(1)}, u32[]{:S(2)}, u32[]{:S(2)}) collective-permute-start(f32[256,512]{0,1:T(8,128)} %collective-permute-done), channel_id=1, source_target_pairs={{0,2},{1,3},{2,4},{3,5},{4,6},{5,7},{6,8},{7,9},{8,10},{9,11},{10,... | collective-permute-start | bytes 1572872 | tf_op jit(solution)/shard_map/ppermute | solution.py:105
  29.1 15.5 %collective-permute-start.5 = (f32[256,512]{0,1:T(8,128)}, f32[256,512]{0,1:T(8,128)S(1)}, u32[]{:S(2)}, u32[]{:S(2)}) collective-permute-start(f32[256,512]{0,1:T(8,128)} %collective-permute-done.4), channel_id=1, source_target_pairs={{0,14},{1,15},{2,0},{3,1},{4,2},{5,3},{6,4},{7,5},{8,6},{9,7},{10,... | collective-permute-start | bytes 1572872 | tf_op jit(solution)/shard_map/ppermute | solution.py:106
  42.7 15.0 %collective-permute-start.2 = (f32[256,512]{0,1:T(8,128)S(1)}, f32[256,512]{0,1:T(8,128)S(1)}, u32[]{:S(2)}, u32[]{:S(2)}) collective-permute-start(f32[256,512]{0,1:T(8,128)S(1)} %collective-permute-done.1), channel_id=1, source_target_pairs={{0,2},{1,3},{2,4},{3,5},{4,6},{5,7},{6,8},{7,9},{8,10},{9,11},{10,... | collective-permute-start | bytes 1572872 | tf_op jit(solution)/shard_map/ppermute | solution.py:105
  44.6 15.8 %collective-permute-start.6 = (f32[256,512]{0,1:T(8,128)S(1)}, f32[256,512]{0,1:T(8,128)S(1)}, u32[]{:S(2)}, u32[]{:S(2)}) collective-permute-start(f32[256,512]{0,1:T(8,128)S(1)} %collective-permute-done.5), channel_id=1, source_target_pairs={{0,14},{1,15},{2,0},{3,1},{4,2},{5,3},{6,4},{7,5},{8,6},{9,7},{10,... | collective-permute-start | bytes 1572872 | tf_op jit(solution)/shard_map/ppermute | solution.py:106
  49.2 32.9 %collective-permute-start.9 = (f32[256,512]{0,1:T(8,128)}, f32[256,512]{0,1:T(8,128)S(1)}, u32[]{:S(2)}, u32[]{:S(2)}) collective-permute-start(f32[256,512]{0,1:T(8,128)} %collective-permute-done), channel_id=1, source_target_pairs={{0,1},{1,0},{2,3},{3,2},{4,5},{5,4},{6,7},{7,6},{8,9},{9,8},{10,11... | collective-permute-start | bytes 1572872 | tf_op jit(solution)/shard_map/ppermute | solution.py:113
  53.8 37.7 %collective-permute-start.15 = (f32[256,512]{0,1:T(8,128)}, f32[256,512]{0,1:T(8,128)S(1)}, u32[]{:S(2)}, u32[]{:S(2)}) collective-permute-start(f32[256,512]{0,1:T(8,128)} %collective-permute-done.4), channel_id=1, source_target_pairs={{0,1},{1,0},{2,3},{3,2},{4,5},{5,4},{6,7},{7,6},{8,9},{9,8},{10,11... | collective-permute-start | bytes 1572872 | tf_op jit(solution)/shard_map/ppermute | solution.py:113
  57.6 8.3 %collective-permute-start.3 = (f32[128,512]{0,1:T(8,128)S(1)}, f32[128,512]{0,1:T(8,128)S(1)}, u32[]{:S(2)}, u32[]{:S(2)}) collective-permute-start(f32[128,512]{0,1:T(8,128)S(1)} %slice.66), channel_id=1, source_target_pairs={{0,2},{1,3},{2,4},{3,5},{4,6},{5,7},{6,8},{7,9},{8,10},{9,11},{10,... | collective-permute-start | bytes 786440 | tf_op jit(solution)/shard_map/ppermute | solution.py:110
  60.4 11.1 %collective-permute-start.7 = (f32[128,512]{0,1:T(8,128)S(1)}, f32[128,512]{0,1:T(8,128)S(1)}, u32[]{:S(2)}, u32[]{:S(2)}) collective-permute-start(f32[128,512]{0,1:T(8,128)S(1)} %slice.67), channel_id=1, source_target_pairs={{0,14},{1,15},{2,0},{3,1},{4,2},{5,3},{6,4},{7,5},{8,6},{9,7},{10,... | collective-permute-start | bytes 786440 | tf_op jit(solution)/shard_map/ppermute | solution.py:111
  66.0 19.3 %collective-permute-start.10 = (f32[256,512]{0,1:T(8,128)S(1)}, f32[256,512]{0,1:T(8,128)S(1)}, u32[]{:S(2)}, u32[]{:S(2)}) collective-permute-start(f32[256,512]{0,1:T(8,128)S(1)} %collective-permute-done.1), channel_id=1, source_target_pairs={{0,1},{1,0},{2,3},{3,2},{4,5},{5,4},{6,7},{7,6},{8,9},{9,8},{10,11... | collective-permute-start | bytes 1572872 | tf_op jit(solution)/shard_map/ppermute | solution.py:113
  71.5 19.2 %collective-permute-start.14 = (f32[256,512]{0,1:T(8,128)S(1)}, f32[256,512]{0,1:T(8,128)S(1)}, u32[]{:S(2)}, u32[]{:S(2)}) collective-permute-start(f32[256,512]{0,1:T(8,128)S(1)} %collective-permute-done.5), channel_id=1, source_target_pairs={{0,1},{1,0},{2,3},{3,2},{4,5},{5,4},{6,7},{7,6},{8,9},{9,8},{10,11... | collective-permute-start | bytes 1572872 | tf_op jit(solution)/shard_map/ppermute | solution.py:113
  78.2 9.9 %collective-permute-start.11 = (f32[256,512]{0,1:T(8,128)S(1)}, f32[256,512]{0,1:T(8,128)S(1)}, u32[]{:S(2)}, u32[]{:S(2)}) collective-permute-start(f32[256,512]{0,1:T(8,128)S(1)} %collective-permute-done.2), channel_id=1, source_target_pairs={{0,1},{1,0},{2,3},{3,2},{4,5},{5,4},{6,7},{7,6},{8,9},{9,8},{10,11... | collective-permute-start | bytes 1572872 | tf_op jit(solution)/shard_map/ppermute | solution.py:113
  82.2 6.9 %collective-permute-start.12 = (f32[256,512]{0,1:T(8,128)S(1)}, f32[256,512]{0,1:T(8,128)S(1)}, u32[]{:S(2)}, u32[]{:S(2)}) collective-permute-start(f32[256,512]{0,1:T(8,128)S(1)} %constant_dynamic-update-slice_fusion), channel_id=1, source_target_pairs={{0,1},{1,0},{2,3},{3,2},{4,5},{5,4},{6,7},{7,6},{8,9},{9,8},{10,11... | collective-permute-start | bytes 1572872 | tf_op jit(solution)/shard_map/ppermute | solution.py:113
  85.3 4.6 %collective-permute-start.13 = (f32[256,512]{0,1:T(8,128)S(1)}, f32[256,512]{0,1:T(8,128)S(1)}, u32[]{:S(2)}, u32[]{:S(2)}) collective-permute-start(f32[256,512]{0,1:T(8,128)S(1)} %collective-permute-done.6), channel_id=1, source_target_pairs={{0,1},{1,0},{2,3},{3,2},{4,5},{5,4},{6,7},{7,6},{8,9},{9,8},{10,11... | collective-permute-start | bytes 1572872 | tf_op jit(solution)/shard_map/ppermute | solution.py:113
  184.0 5.5 %copy-start = (f32[6,256,512]{2,1,0:T(8,128)S(1)}, f32[6,256,512]{2,1,0:T(8,128)}, u32[]{:S(2)}) copy-start(f32[6,256,512]{2,1,0:T(8,128)} %copy.15) | copy-start | bytes 9437188
  184.0 8.4 %copy-start.1 = (f32[1,256,1536]{2,1,0:T(8,128)S(1)}, f32[1,256,1536]{2,1,0:T(8,128)}, u32[]{:S(2)}) copy-start(f32[1,256,1536]{2,1,0:T(8,128)} %get-tuple-element.12) | copy-start | bytes 4718596
  184.0 8.4 %copy-start.2 = (f32[1,256,1536]{2,1,0:T(8,128)S(1)}, f32[1,256,1536]{2,1,0:T(8,128)}, u32[]{:S(2)}) copy-start(f32[1,256,1536]{2,1,0:T(8,128)} %get-tuple-element.13) | copy-start | bytes 4718596

commit v3 on v0

--- a/solution.py
+++ b/solution.py
@@ -20,19 +20,34 @@
         lo = kb * nb
         p_ref[...] = o_ref[lo:lo + nb, lo:lo + nb]
 
-        def step(j, carry):
+        def step(i, carry):
+            j = 2 * i
             block = p_ref[...]
-            row = p_ref[pl.ds(j, 1), :]
-            piv = jnp.sum(jnp.where(lane_r == j, row, 0.0), axis=1, keepdims=True)
-            inv = 1.0 / piv
-            rnew = jnp.where(lane_r == j, 1.0, row) * inv
-            col = jnp.sum(jnp.where(lane_p == j, block, 0.0), axis=1, keepdims=True)
-            col = jnp.where(sub_c == j, 0.0, col)
-            p_ref[...] = jnp.where(lane_p == j, 0.0, block) - col * rnew
-            p_ref[pl.ds(j, 1), :] = rnew
+            pair = p_ref[pl.ds(j, 2), :]
+            r0 = pair[0:1, :]
+            r1 = pair[1:2, :]
+            at0 = lane_r == j
+            at1 = lane_r == j + 1
+            e00 = jnp.sum(jnp.where(at0, r0, 0.0), axis=1, keepdims=True)
+            e01 = jnp.sum(jnp.where(at1, r0, 0.0), axis=1, keepdims=True)
+            e10 = jnp.sum(jnp.where(at0, r1, 0.0), axis=1, keepdims=True)
+            e11 = jnp.sum(jnp.where(at1, r1, 0.0), axis=1, keepdims=True)
+            inv_det = 1.0 / (e00 * e11 - e01 * e10)
+            m0 = jnp.where(at0, 1.0, jnp.where(at1, 0.0, r0))
+            m1 = jnp.where(at0, 0.0, jnp.where(at1, 1.0, r1))
+            n0 = (e11 * m0 - e01 * m1) * inv_det
+            n1 = (e00 * m1 - e10 * m0) * inv_det
+            in_pair = jnp.logical_or(sub_c == j, sub_c == j + 1)
+            c0 = jnp.sum(jnp.where(lane_p == j, block, 0.0), axis=1, keepdims=True)
+            c1 = jnp.sum(jnp.where(lane_p == j + 1, block, 0.0), axis=1, keepdims=True)
+            c0 = jnp.where(in_pair, 0.0, c0)
+            c1 = jnp.where(in_pair, 0.0, c1)
+            cut = jnp.logical_or(lane_p == j, lane_p == j + 1)
+            p_ref[...] = jnp.where(cut, 0.0, block) - c0 * n0 - c1 * n1
+            p_ref[pl.ds(j, 2), :] = jnp.concatenate([n0, n1], 0)
             return carry
 
-        lax.fori_loop(0, nb, step, 0)
+        lax.fori_loop(0, nb // 2, step, 0)
         pinv = p_ref[...]
         lane_n = lax.broadcasted_iota(jnp.int32, (nb, n), 1)
         sub_n = lax.broadcasted_iota(jnp.int32, (nb, n), 0)

time: 195 us -> 195 us (level)
  no operation moved by 1% of the time
where the time goes in v3:
time: 195 us; the launch traced here: 194 us
  Pallas kernels  58.7 us (30%)
  starting transfers between devices  56.4 us (29%)
  local copies, waits for them, and re-layouts  40.6 us (21%)
  matrix products  15.7 us (8%)
  waiting for transfers between devices  12.1 us (6%)
  other arithmetic  9.67 us (5%)
    pallas_call x1, Pallas kernels, spd_inverse(): pl.pallas_call(_gj_kernel, out_shape=jax.ShapeDtypeStruct((n, n), jnp.flo...  58.7 us
    ppermute x8, starting transfers between devices, ring_gather(): sib = [lax.ppermute(piece, AXES, swap) for piece in rel]  23.5 us
    ppermute x3, starting transfers between devices, ring_gather(): b = lax.ppermute(b, AXES, ccw)  17.7 us
    unnamed x25, local copies, waits for them, and re-layouts  14.9 us
    ppermute x3, waiting for transfers between devices, ring_gather(): a = lax.ppermute(a, AXES, cw)  11.9 us
    ppermute x3, starting transfers between devices, ring_gather(): a = lax.ppermute(a, AXES, cw)  8.64 us
    gather x1, local copies, waits for them, and re-layouts, ring_gather(): full = jnp.take(stacked, idx, axis=0)  7.69 us
    slice x2, local copies, waits for them, and re-layouts, body(): first_ext = g_a[:outer]  5.36 us
  transfers between devices with their start and end apart: 16, of which 3 were waited for; matrix products, arithmetic and copies ran while one was open for 10% of the time, Pallas kernels for 0%

profile of v3, /device:TPU:1, one launch (start us, length us, event | category | flops | bytes accessed | tf_op | source)
XLA Modules:
  0.0 193.6 jit_solution(8257203560120482196)
XLA Ops:
  0.0 0.9 compare_select_fusion
  0.9 1.1 slice.65
  2.0 0.2 copy.9
  2.2 1.6 gather_fusion
  3.8 0.1 bitcast_select_fusion.1
  3.9 4.8 %collective-permute-start = (f32[256,512]{0,1:T(8,128)S(1)}, f32[256,512]{0,1:T(8,128)}, u32[]{:S(2)}, u32[]{:S(2)}) collective-permute-start(f32[256,512]{0,1:T(8,128)S(1)} %bitcast_select_fusion.1), channel_id=1, source_target_pairs={{0,2},{1,3},{2,4},{3,5},{4,6},{5,7},{6,8},{7,9},{8,10},{9,11},{10,... | collective-permute-start | bytes 1572872 | tf_op jit(solution)/shard_map/ppermute | solution.py:101
  8.7 8.6 %collective-permute-start.4 = (f32[256,512]{0,1:T(8,128)S(1)}, f32[256,512]{0,1:T(8,128)}, u32[]{:S(2)}, u32[]{:S(2)}) collective-permute-start(f32[256,512]{0,1:T(8,128)S(1)} %bitcast_select_fusion.1), channel_id=1, source_target_pairs={{0,14},{1,15},{2,0},{3,1},{4,2},{5,3},{6,4},{7,5},{8,6},{9,7},{10,... | collective-permute-start | bytes 1572872 | tf_op jit(solution)/shard_map/ppermute | solution.py:102
  17.3 2.9 %collective-permute-start.8 = (f32[256,512]{0,1:T(8,128)S(1)}, f32[256,512]{0,1:T(8,128)}, u32[]{:S(2)}, u32[]{:S(2)}) collective-permute-start(f32[256,512]{0,1:T(8,128)S(1)} %bitcast_select_fusion.1), channel_id=1, source_target_pairs={{0,1},{1,0},{2,3},{3,2},{4,5},{5,4},{6,7},{7,6},{8,9},{9,8},{10,11... | collective-permute-start | bytes 1572872 | tf_op jit(solution)/shard_map/ppermute | solution.py:109
  20.3 0.8 constant_dynamic-slice_fusion.1
  21.1 1.9 select_bitcast_fusion.1
  23.0 0.1 copy.10
  23.1 0.1 reshape.235
  23.2 3.9 %collective-permute-done = f32[256,512]{0,1:T(8,128)} collective-permute-done((f32[256,512]{0,1:T(8,128)S(1)}, f32[256,512]{0,1:T(8,128)}, u32[]{:S(2)}, u32[]{:S(2)}) %collective-permute-start) | collective-permute-done | bytes 524320 | tf_op jit(solution)/shard_map/ppermute | solution.py:101
  27.1 1.9 collective-permute-start.1
  29.1 0.1 reshape.234
  29.1 0.0 collective-permute-done.4
  29.1 4.6 %collective-permute-start.5 = (f32[256,512]{0,1:T(8,128)}, f32[256,512]{0,1:T(8,128)S(1)}, u32[]{:S(2)}, u32[]{:S(2)}) collective-permute-start(f32[256,512]{0,1:T(8,128)} %collective-permute-done.4), channel_id=1, source_target_pairs={{0,14},{1,15},{2,0},{3,1},{4,2},{5,3},{6,4},{7,5},{8,6},{9,7},{10,... | collective-permute-start | bytes 1572872 | tf_op jit(solution)/shard_map/ppermute | solution.py:102
  33.7 0.9 fusion.1
  34.7 8.0 %collective-permute-done.1 = f32[256,512]{0,1:T(8,128)S(1)} collective-permute-done((f32[256,512]{0,1:T(8,128)}, f32[256,512]{0,1:T(8,128)S(1)}, u32[]{:S(2)}, u32[]{:S(2)}) %collective-permute-start.1) | collective-permute-done | bytes 524320 | tf_op jit(solution)/shard_map/ppermute | solution.py:101
  42.7 1.9 collective-permute-start.2
  44.6 0.0 collective-permute-done.5
  44.6 4.6 %collective-permute-start.6 = (f32[256,512]{0,1:T(8,128)S(1)}, f32[256,512]{0,1:T(8,128)S(1)}, u32[]{:S(2)}, u32[]{:S(2)}) collective-permute-start(f32[256,512]{0,1:T(8,128)S(1)} %collective-permute-done.5), channel_id=1, source_target_pairs={{0,14},{1,15},{2,0},{3,1},{4,2},{5,3},{6,4},{7,5},{8,6},{9,7},{10,... | collective-permute-start | bytes 1572872 | tf_op jit(solution)/shard_map/ppermute | solution.py:102
  49.2 4.6 %collective-permute-start.9 = (f32[256,512]{0,1:T(8,128)}, f32[256,512]{0,1:T(8,128)S(1)}, u32[]{:S(2)}, u32[]{:S(2)}) collective-permute-start(f32[256,512]{0,1:T(8,128)} %collective-permute-done), channel_id=1, source_target_pairs={{0,1},{1,0},{2,3},{3,2},{4,5},{5,4},{6,7},{7,6},{8,9},{9,8},{10,11... | collective-permute-start | bytes 1572872 | tf_op jit(solution)/shard_map/ppermute | solution.py:109
  53.8 1.9 collective-permute-start.15
  55.7 1.9 bitcast_dynamic-update-slice_fusion.14
  57.6 1.9 collective-permute-start.3
  59.6 0.8 bitcast_dynamic-update-slice_fusion.13
  60.4 4.6 %collective-permute-start.7 = (f32[128,512]{0,1:T(8,128)S(1)}, f32[128,512]{0,1:T(8,128)S(1)}, u32[]{:S(2)}, u32[]{:S(2)}) collective-permute-start(f32[128,512]{0,1:T(8,128)S(1)} %slice.67), channel_id=1, source_target_pairs={{0,14},{1,15},{2,0},{3,1},{4,2},{5,3},{6,4},{7,5},{8,6},{9,7},{10,... | collective-permute-start | bytes 786440 | tf_op jit(solution)/shard_map/ppermute | solution.py:107
  65.0 0.8 bitcast_dynamic-update-slice_fusion.12
  65.8 0.1 collective-permute-done.3
  66.0 5.5 %collective-permute-start.10 = (f32[256,512]{0,1:T(8,128)S(1)}, f32[256,512]{0,1:T(8,128)S(1)}, u32[]{:S(2)}, u32[]{:S(2)}) collective-permute-start(f32[256,512]{0,1:T(8,128)S(1)} %collective-permute-done.1), channel_id=1, source_target_pairs={{0,1},{1,0},{2,3},{3,2},{4,5},{5,4},{6,7},{7,6},{8,9},{9,8},{10,11... | collective-permute-start | bytes 1572872 | tf_op jit(solution)/shard_map/ppermute | solution.py:109
  71.5 2.3 %collective-permute-start.14 = (f32[256,512]{0,1:T(8,128)S(1)}, f32[256,512]{0,1:T(8,128)S(1)}, u32[]{:S(2)}, u32[]{:S(2)}) collective-permute-start(f32[256,512]{0,1:T(8,128)S(1)} %collective-permute-done.5), channel_id=1, source_target_pairs={{0,1},{1,0},{2,3},{3,2},{4,5},{5,4},{6,7},{7,6},{8,9},{9,8},{10,11... | collective-permute-start | bytes 1572872 | tf_op jit(solution)/shard_map/ppermute | solution.py:109
  73.9 0.8 bitcast_dynamic-update-slice_fusion.11
  74.7 0.8 bitcast_dynamic-update-slice_fusion.10
  75.5 0.8 bitcast_dynamic-update-slice_fusion.9
  76.4 1.9 bitcast_dynamic-update-slice_fusion.8
  78.2 2.0 %collective-permute-start.11 = (f32[256,512]{0,1:T(8,128)S(1)}, f32[256,512]{0,1:T(8,128)S(1)}, u32[]{:S(2)}, u32[]{:S(2)}) collective-permute-start(f32[256,512]{0,1:T(8,128)S(1)} %collective-permute-done.2), channel_id=1, source_target_pairs={{0,1},{1,0},{2,3},{3,2},{4,5},{5,4},{6,7},{7,6},{8,9},{9,8},{10,11... | collective-permute-start | bytes 1572872 | tf_op jit(solution)/shard_map/ppermute | solution.py:109
  80.3 1.9 bitcast_dynamic-update-slice_fusion.7
  82.2 2.3 %collective-permute-start.12 = (f32[256,512]{0,1:T(8,128)S(1)}, f32[256,512]{0,1:T(8,128)S(1)}, u32[]{:S(2)}, u32[]{:S(2)}) collective-permute-start(f32[256,512]{0,1:T(8,128)S(1)} %constant_dynamic-update-slice_fusion), channel_id=1, source_target_pairs={{0,1},{1,0},{2,3},{3,2},{4,5},{5,4},{6,7},{7,6},{8,9},{9,8},{10,11... | collective-permute-start | bytes 1572872 | tf_op jit(solution)/shard_map/ppermute | solution.py:109
  84.4 0.8 bitcast_dynamic-update-slice_fusion.6
  85.3 2.0 %collective-permute-start.13 = (f32[256,512]{0,1:T(8,128)S(1)}, f32[256,512]{0,1:T(8,128)S(1)}, u32[]{:S(2)}, u32[]{:S(2)}) collective-permute-start(f32[256,512]{0,1:T(8,128)S(1)} %collective-permute-done.6), channel_id=1, source_target_pairs={{0,1},{1,0},{2,3},{3,2},{4,5},{5,4},{6,7},{7,6},{8,9},{9,8},{10,11... | collective-permute-start | bytes 1572872 | tf_op jit(solution)/shard_map/ppermute | solution.py:109
  87.3 0.8 bitcast_dynamic-update-slice_fusion.5
  88.2 0.8 bitcast_dynamic-update-slice_fusion.4
  89.0 0.8 bitcast_dynamic-update-slice_fusion.3
  89.9 0.8 bitcast_dynamic-update-slice_fusion.2
  90.7 0.8 bitcast_dynamic-update-slice_fusion.1
  91.5 0.9 bitcast_dynamic-update-slice_fusion
  92.4 7.7 %gather_fusion.1 = f32[16,256,512]{1,2,0:T(8,128)} fusion(f32[16,256,512]{1,2,0:T(8,128)} %bitcast_dynamic-update-slice_fusion, s32[1024]{0:T(1024)S(1)} %pad_clamp_fusion.2), kind=kCustom, calls=%fused_computation.3 | custom fusion | bytes 16777280 | tf_op jit(solution)/shard_map/jit(_take)/gather | solution.py:117
  100.1 4.2 %broadcast_select_fusion = f32[16,256,512]{1,2,0:T(8,128)S(1)} fusion(f32[16,256,512]{1,2,0:T(8,128)} %gather_fusion.1, pred[16]{0:T(512)(128)(4,1)S(1)} %compare_and_fusion.2), kind=kLoop, calls=%fused_computation.4 | loop fusion | flops 2097152 | bytes 16777232 | tf_op jit(solution)/shard_map/jit(_take)/select_n | solution.py:117
  104.4 0.1 fusion.15
  104.5 3.0 %fusion.14 = (f32[6,256,512]{1,2,0:T(8,128)}, f32[6,256,512]{1,2,0:T(8,128)}) fusion(f32[16,256,512]{1,2,0:T(8,128)S(1)} %broadcast_select_fusion), kind=kLoop, calls=%fused_computation.70 | loop fusion | bytes 12582912 | tf_op jit(solution)/shard_map/slice | solution.py:143
  107.5 0.3 copy.12
  107.8 0.3 copy.13
  108.2 1.8 gather_fusion.2
  110.0 1.6 gather_fusion.3
  111.6 3.1 %fusion.13.a_ref = f32[512,512]{1,0:T(8,128)} fusion(f32[512,512]{1,0:T(8,128)S(1)} %gather_fusion.3, f32[512,512]{1,0:T(8,128)S(1)} %gather_fusion.2, pred[512]{0:T(512)(128)(4,1)S(1)} %get-tuple-element.22, pred[512]{0:T(512)(128)(4,1)S(1)} %get-tuple-element.23), kind=kOutput, calls=%fused_computation.69 | convolution fusion | flops 1611399168 | bytes 3146752 | tf_op jit(solution)/shard_map/dot_general | solution.py:141
  114.7 58.7 %shard_map.28 = f32[512,512]{1,0:T(8,128)} custom-call(f32[512,512]{1,0:T(8,128)} %fusion.13.a_ref), custom_call_target="tpu_custom_call" | custom-call | flops 1610612736 | bytes 2097152 | tf_op jit(solution)/shard_map/pallas_call | solution.py:68
  173.5 4.2 %fusion.12 = f32[512,512]{1,0:T(8,128)} fusion(f32[512,512]{1,0:T(8,128)} %shard_map.28, f32[512,512]{1,0:T(8,128)S(1)} %gather_fusion.3, f32[512,512]{1,0:T(8,128)S(1)} %gather_fusion.2, pred[512]{0:T(512)(128)(4,1)S(1)} %get-tuple-element.22, pred[512]{0:T(512)(128)(4,1)S(1)} %get-tuple-element.23), kind=kOutput, calls=%fused_computation.68 | convolution fusion | flops 1611399168 | bytes 4195328 | tf_op jit(solution)/shard_map/dot_general | solution.py:142
  177.7 2.4 %copy.14 = f32[6,256,512]{2,1,0:T(8,128)S(1)} copy(f32[6,256,512]{1,2,0:T(8,128)} %get-tuple-element.8) | data formatting | bytes 6291456 | tf_op jit(solution)/shard_map/slice | solution.py:143
  180.1 3.6 %copy.15 = f32[6,256,512]{2,1,0:T(8,128)} copy(f32[6,256,512]{1,2,0:T(8,128)} %get-tuple-element.9) | data formatting | bytes 6291456 | tf_op jit(solution)/shard_map/slice | solution.py:144
  183.7 2.7 %fusion.2 = f32[256,512]{1,0:T(8,128)S(1)} fusion(f32[512,512]{1,0:T(8,128)} %fusion.12, f32[256,512]{0,1:T(8,128)} %copy-done.4, s32[256]{0:T(256)S(1)} %fusion.9, s32[512]{0:T(512)S(1)} %bitcast.71, pred[256]{0:T(512)(128)(4,1)S(1)} %get-tuple-element.20), kind=kOutput, calls=%fused_computation.30 | convolution fusion | flops 805699584 | bytes 2100480 | tf_op jit(solution)/shard_map/dot_general | solution.py:154
  186.4 2.8 %convolution_bitcast_fusion.1 = f32[1,256,1536]{2,1,0:T(8,128)S(1)} fusion(f32[256,512]{1,0:T(8,128)S(1)} %fusion.2, f32[1536,512]{1,0:T(8,128)S(1)} %bitcast.66), kind=kOutput, calls=%fused_computation.8 | convolution fusion | flops 2415919104 | bytes 5242880 | tf_op jit(solution)/shard_map/dot_general | solution.py:156
  189.2 2.8 %convolution_bitcast_fusion = f32[1,256,1536]{2,1,0:T(8,128)S(1)} fusion(f32[256,512]{1,0:T(8,128)S(1)} %fusion.2, f32[1536,512]{1,0:T(8,128)S(1)} %bitcast.67), kind=kOutput, calls=%fused_computation.7 | convolution fusion | flops 2415919104 | bytes 5242880 | tf_op jit(solution)/shard_map/dot_general | solution.py:157
  192.1 1.5 fusion
  (38 shorter events, 0.2 us)
Async XLA Ops:
  0.0 21.1 %copy-start.3 = (f32[1,256,2048]{2,1,0:T(8,128)S(1)}, f32[1,256,2048]{2,1,0:T(8,128)}, u32[]{:S(2)}) copy-start(f32[1,256,2048]{2,1,0:T(8,128)} %param.4) | copy-start | bytes 6291460
  3.9 81.4 %copy-start.4 = (f32[256,512]{0,1:T(8,128)}, f32[256,512]{0,1:T(8,128)S(1)}, u32[]{:S(2)}) copy-start(f32[256,512]{0,1:T(8,128)S(1)} %bitcast_select_fusion.1) | copy-start | bytes 1572868
  3.9 23.2 %collective-permute-start = (f32[256,512]{0,1:T(8,128)S(1)}, f32[256,512]{0,1:T(8,128)}, u32[]{:S(2)}, u32[]{:S(2)}) collective-permute-start(f32[256,512]{0,1:T(8,128)S(1)} %bitcast_select_fusion.1), channel_id=1, source_target_pairs={{0,2},{1,3},{2,4},{3,5},{4,6},{5,7},{6,8},{7,9},{8,10},{9,11},{10,... | collective-permute-start | bytes 1572872 | tf_op jit(solution)/shard_map/ppermute | solution.py:101
  8.7 20.4 %collective-permute-start.4 = (f32[256,512]{0,1:T(8,128)S(1)}, f32[256,512]{0,1:T(8,128)}, u32[]{:S(2)}, u32[]{:S(2)}) collective-permute-start(f32[256,512]{0,1:T(8,128)S(1)} %bitcast_select_fusion.1), channel_id=1, source_target_pairs={{0,14},{1,15},{2,0},{3,1},{4,2},{5,3},{6,4},{7,5},{8,6},{9,7},{10,... | collective-permute-start | bytes 1572872 | tf_op jit(solution)/shard_map/ppermute | solution.py:102
  17.3 60.9 %collective-permute-start.8 = (f32[256,512]{0,1:T(8,128)S(1)}, f32[256,512]{0,1:T(8,128)}, u32[]{:S(2)}, u32[]{:S(2)}) collective-permute-start(f32[256,512]{0,1:T(8,128)S(1)} %bitcast_select_fusion.1), channel_id=1, source_target_pairs={{0,1},{1,0},{2,3},{3,2},{4,5},{5,4},{6,7},{7,6},{8,9},{9,8},{10,11... | collective-permute-start | bytes 1572872 | tf_op jit(solution)/shard_map/ppermute | solution.py:109
  27.1 15.5 %collective-permute-start.1 = (f32[256,512]{0,1:T(8,128)}, f32[256,512]{0,1:T(8,128)S(1)}, u32[]{:S(2)}, u32[]{:S(2)}) collective-permute-start(f32[256,512]{0,1:T(8,128)} %collective-permute-done), channel_id=1, source_target_pairs={{0,2},{1,3},{2,4},{3,5},{4,6},{5,7},{6,8},{7,9},{8,10},{9,11},{10,... | collective-permute-start | bytes 1572872 | tf_op jit(solution)/shard_map/ppermute | solution.py:101
  29.1 15.5 %collective-permute-start.5 = (f32[256,512]{0,1:T(8,128)}, f32[256,512]{0,1:T(8,128)S(1)}, u32[]{:S(2)}, u32[]{:S(2)}) collective-permute-start(f32[256,512]{0,1:T(8,128)} %collective-permute-done.4), channel_id=1, source_target_pairs={{0,14},{1,15},{2,0},{3,1},{4,2},{5,3},{6,4},{7,5},{8,6},{9,7},{10,... | collective-permute-start | bytes 1572872 | tf_op jit(solution)/shard_map/ppermute | solution.py:102
  42.7 15.0 %collective-permute-start.2 = (f32[256,512]{0,1:T(8,128)S(1)}, f32[256,512]{0,1:T(8,128)S(1)}, u32[]{:S(2)}, u32[]{:S(2)}) collective-permute-start(f32[256,512]{0,1:T(8,128)S(1)} %collective-permute-done.1), channel_id=1, source_target_pairs={{0,2},{1,3},{2,4},{3,5},{4,6},{5,7},{6,8},{7,9},{8,10},{9,11},{10,... | collective-permute-start | bytes 1572872 | tf_op jit(solution)/shard_map/ppermute | solution.py:101
  44.6 15.8 %collective-permute-start.6 = (f32[256,512]{0,1:T(8,128)S(1)}, f32[256,512]{0,1:T(8,128)S(1)}, u32[]{:S(2)}, u32[]{:S(2)}) collective-permute-start(f32[256,512]{0,1:T(8,128)S(1)} %collective-permute-done.5), channel_id=1, source_target_pairs={{0,14},{1,15},{2,0},{3,1},{4,2},{5,3},{6,4},{7,5},{8,6},{9,7},{10,... | collective-permute-start | bytes 1572872 | tf_op jit(solution)/shard_map/ppermute | solution.py:102
  49.2 32.9 %collective-permute-start.9 = (f32[256,512]{0,1:T(8,128)}, f32[256,512]{0,1:T(8,128)S(1)}, u32[]{:S(2)}, u32[]{:S(2)}) collective-permute-start(f32[256,512]{0,1:T(8,128)} %collective-permute-done), channel_id=1, source_target_pairs={{0,1},{1,0},{2,3},{3,2},{4,5},{5,4},{6,7},{7,6},{8,9},{9,8},{10,11... | collective-permute-start | bytes 1572872 | tf_op jit(solution)/shard_map/ppermute | solution.py:109
  53.8 37.7 %collective-permute-start.15 = (f32[256,512]{0,1:T(8,128)}, f32[256,512]{0,1:T(8,128)S(1)}, u32[]{:S(2)}, u32[]{:S(2)}) collective-permute-start(f32[256,512]{0,1:T(8,128)} %collective-permute-done.4), channel_id=1, source_target_pairs={{0,1},{1,0},{2,3},{3,2},{4,5},{5,4},{6,7},{7,6},{8,9},{9,8},{10,11... | collective-permute-start | bytes 1572872 | tf_op jit(solution)/shard_map/ppermute | solution.py:109
  57.6 8.3 %collective-permute-start.3 = (f32[128,512]{0,1:T(8,128)S(1)}, f32[128,512]{0,1:T(8,128)S(1)}, u32[]{:S(2)}, u32[]{:S(2)}) collective-permute-start(f32[128,512]{0,1:T(8,128)S(1)} %slice.66), channel_id=1, source_target_pairs={{0,2},{1,3},{2,4},{3,5},{4,6},{5,7},{6,8},{7,9},{8,10},{9,11},{10,... | collective-permute-start | bytes 786440 | tf_op jit(solution)/shard_map/ppermute | solution.py:106
  60.4 11.1 %collective-permute-start.7 = (f32[128,512]{0,1:T(8,128)S(1)}, f32[128,512]{0,1:T(8,128)S(1)}, u32[]{:S(2)}, u32[]{:S(2)}) collective-permute-start(f32[128,512]{0,1:T(8,128)S(1)} %slice.67), channel_id=1, source_target_pairs={{0,14},{1,15},{2,0},{3,1},{4,2},{5,3},{6,4},{7,5},{8,6},{9,7},{10,... | collective-permute-start | bytes 786440 | tf_op jit(solution)/shard_map/ppermute | solution.py:107
  66.0 19.3 %collective-permute-start.10 = (f32[256,512]{0,1:T(8,128)S(1)}, f32[256,512]{0,1:T(8,128)S(1)}, u32[]{:S(2)}, u32[]{:S(2)}) collective-permute-start(f32[256,512]{0,1:T(8,128)S(1)} %collective-permute-done.1), channel_id=1, source_target_pairs={{0,1},{1,0},{2,3},{3,2},{4,5},{5,4},{6,7},{7,6},{8,9},{9,8},{10,11... | collective-permute-start | bytes 1572872 | tf_op jit(solution)/shard_map/ppermute | solution.py:109
  71.5 19.2 %collective-permute-start.14 = (f32[256,512]{0,1:T(8,128)S(1)}, f32[256,512]{0,1:T(8,128)S(1)}, u32[]{:S(2)}, u32[]{:S(2)}) collective-permute-start(f32[256,512]{0,1:T(8,128)S(1)} %collective-permute-done.5), channel_id=1, source_target_pairs={{0,1},{1,0},{2,3},{3,2},{4,5},{5,4},{6,7},{7,6},{8,9},{9,8},{10,11... | collective-permute-start | bytes 1572872 | tf_op jit(solution)/shard_map/ppermute | solution.py:109
  78.2 9.9 %collective-permute-start.11 = (f32[256,512]{0,1:T(8,128)S(1)}, f32[256,512]{0,1:T(8,128)S(1)}, u32[]{:S(2)}, u32[]{:S(2)}) collective-permute-start(f32[256,512]{0,1:T(8,128)S(1)} %collective-permute-done.2), channel_id=1, source_target_pairs={{0,1},{1,0},{2,3},{3,2},{4,5},{5,4},{6,7},{7,6},{8,9},{9,8},{10,11... | collective-permute-start | bytes 1572872 | tf_op jit(solution)/shard_map/ppermute | solution.py:109
  82.2 6.9 %collective-permute-start.12 = (f32[256,512]{0,1:T(8,128)S(1)}, f32[256,512]{0,1:T(8,128)S(1)}, u32[]{:S(2)}, u32[]{:S(2)}) collective-permute-start(f32[256,512]{0,1:T(8,128)S(1)} %constant_dynamic-update-slice_fusion), channel_id=1, source_target_pairs={{0,1},{1,0},{2,3},{3,2},{4,5},{5,4},{6,7},{7,6},{8,9},{9,8},{10,11... | collective-permute-start | bytes 1572872 | tf_op jit(solution)/shard_map/ppermute | solution.py:109
  85.3 4.6 %collective-permute-start.13 = (f32[256,512]{0,1:T(8,128)S(1)}, f32[256,512]{0,1:T(8,128)S(1)}, u32[]{:S(2)}, u32[]{:S(2)}) collective-permute-start(f32[256,512]{0,1:T(8,128)S(1)} %collective-permute-done.6), channel_id=1, source_target_pairs={{0,1},{1,0},{2,3},{3,2},{4,5},{5,4},{6,7},{7,6},{8,9},{9,8},{10,11... | collective-permute-start | bytes 1572872 | tf_op jit(solution)/shard_map/ppermute | solution.py:109
  183.7 5.5 %copy-start = (f32[6,256,512]{2,1,0:T(8,128)S(1)}, f32[6,256,512]{2,1,0:T(8,128)}, u32[]{:S(2)}) copy-start(f32[6,256,512]{2,1,0:T(8,128)} %copy.15) | copy-start | bytes 9437188
  183.7 8.4 %copy-start.1 = (f32[1,256,1536]{2,1,0:T(8,128)S(1)}, f32[1,256,1536]{2,1,0:T(8,128)}, u32[]{:S(2)}) copy-start(f32[1,256,1536]{2,1,0:T(8,128)} %get-tuple-element.12) | copy-start | bytes 4718596
  183.7 8.4 %copy-start.2 = (f32[1,256,1536]{2,1,0:T(8,128)S(1)}, f32[1,256,1536]{2,1,0:T(8,128)}, u32[]{:S(2)}) copy-start(f32[1,256,1536]{2,1,0:T(8,128)} %get-tuple-element.13) | copy-start | bytes 4718596

commit v4 on v0

--- a/solution.py
+++ b/solution.py
@@ -138,8 +138,8 @@
     base = jnp.concatenate([left_part, right_part], 1)
     solved = jnp.dot(left, sinv, precision=HI)
     contract = (((1,), (1,)), ((), ()))
-    update_first = lax.dot_general(solved, first_ext, contract, precision=lax.Precision.HIGHEST)
-    update_second = lax.dot_general(solved, second_ext, contract, precision=lax.Precision.HIGHEST)
+    update_first = lax.dot_general(solved, first_ext, contract, precision=lax.Precision.HIGH)
+    update_second = lax.dot_general(solved, second_ext, contract, precision=lax.Precision.HIGH)
     merged = base - jnp.concatenate([update_first, update_second], 1)
     return merged.astype(jnp.bfloat16)[None]
 

time: 195 us -> 192 us (0.985)
  matrix products: 15.7 us -> 13.2 us
    dot_general x2, matrix products: 5.68 us -> 3.19 us  [the longest x1 1.65 us: body(): lax.dot_general(solved, second_ext, contract, precision=lax.Precision.HIGH)]
where the time goes in v4:
time: 192 us
  Pallas kernels  59.1 us (31%)
  starting transfers between devices  56.4 us (29%)
  local copies, waits for them, and re-layouts  40.6 us (21%)
  matrix products  13.2 us (7%)
  waiting for transfers between devices  12.1 us (6%)
  other arithmetic  9.67 us (5%)
    pallas_call x1, Pallas kernels, spd_inverse(): pl.pallas_call(_gj_kernel, out_shape=jax.ShapeDtypeStruct((n, n), jnp.flo...  59.1 us
    ppermute x8, starting transfers between devices, ring_gather(): sib = [lax.ppermute(piece, AXES, swap) for piece in rel]  23.5 us
    ppermute x3, starting transfers between devices, ring_gather(): b = lax.ppermute(b, AXES, ccw)  17.7 us
    unnamed x25, local copies, waits for them, and re-layouts  14.9 us
    ppermute x3, waiting for transfers between devices, ring_gather(): a = lax.ppermute(a, AXES, cw)  11.9 us
    ppermute x3, starting transfers between devices, ring_gather(): a = lax.ppermute(a, AXES, cw)  8.64 us
    gather x1, local copies, waits for them, and re-layouts, ring_gather(): full = jnp.take(stacked, idx, axis=0)  7.69 us
    slice x2, local copies, waits for them, and re-layouts, body(): first_ext = g_a[:outer]  5.36 us
  transfers between devices with their start and end apart: 16, of which 3 were waited for; matrix products, arithmetic and copies ran while one was open for 10% of the time, Pallas kernels for 0%

profile of v4, /device:TPU:1, one launch (start us, length us, event | category | flops | bytes accessed | tf_op | source)
XLA Modules:
  0.0 191.5 jit_solution(7519294919029172468)
XLA Ops:
  0.0 0.9 compare_select_fusion
  0.9 1.1 slice.65
  2.0 0.2 copy.9
  2.2 1.6 gather_fusion
  3.8 0.1 bitcast_select_fusion.1
  3.9 4.8 %collective-permute-start = (f32[256,512]{0,1:T(8,128)S(1)}, f32[256,512]{0,1:T(8,128)}, u32[]{:S(2)}, u32[]{:S(2)}) collective-permute-start(f32[256,512]{0,1:T(8,128)S(1)} %bitcast_select_fusion.1), channel_id=1, source_target_pairs={{0,2},{1,3},{2,4},{3,5},{4,6},{5,7},{6,8},{7,9},{8,10},{9,11},{10,... | collective-permute-start | bytes 1572872 | tf_op jit(solution)/shard_map/ppermute | solution.py:86
  8.7 8.6 %collective-permute-start.4 = (f32[256,512]{0,1:T(8,128)S(1)}, f32[256,512]{0,1:T(8,128)}, u32[]{:S(2)}, u32[]{:S(2)}) collective-permute-start(f32[256,512]{0,1:T(8,128)S(1)} %bitcast_select_fusion.1), channel_id=1, source_target_pairs={{0,14},{1,15},{2,0},{3,1},{4,2},{5,3},{6,4},{7,5},{8,6},{9,7},{10,... | collective-permute-start | bytes 1572872 | tf_op jit(solution)/shard_map/ppermute | solution.py:87
  17.3 2.9 %collective-permute-start.8 = (f32[256,512]{0,1:T(8,128)S(1)}, f32[256,512]{0,1:T(8,128)}, u32[]{:S(2)}, u32[]{:S(2)}) collective-permute-start(f32[256,512]{0,1:T(8,128)S(1)} %bitcast_select_fusion.1), channel_id=1, source_target_pairs={{0,1},{1,0},{2,3},{3,2},{4,5},{5,4},{6,7},{7,6},{8,9},{9,8},{10,11... | collective-permute-start | bytes 1572872 | tf_op jit(solution)/shard_map/ppermute | solution.py:94
  20.3 0.8 constant_dynamic-slice_fusion.1
  21.1 1.9 select_bitcast_fusion.1
  23.0 0.1 copy.10
  23.1 0.1 reshape.235
  23.2 3.9 %collective-permute-done = f32[256,512]{0,1:T(8,128)} collective-permute-done((f32[256,512]{0,1:T(8,128)S(1)}, f32[256,512]{0,1:T(8,128)}, u32[]{:S(2)}, u32[]{:S(2)}) %collective-permute-start) | collective-permute-done | bytes 524320 | tf_op jit(solution)/shard_map/ppermute | solution.py:86
  27.1 1.9 collective-permute-start.1
  29.1 0.1 reshape.234
  29.1 0.0 collective-permute-done.4
  29.1 4.6 %collective-permute-start.5 = (f32[256,512]{0,1:T(8,128)}, f32[256,512]{0,1:T(8,128)S(1)}, u32[]{:S(2)}, u32[]{:S(2)}) collective-permute-start(f32[256,512]{0,1:T(8,128)} %collective-permute-done.4), channel_id=1, source_target_pairs={{0,14},{1,15},{2,0},{3,1},{4,2},{5,3},{6,4},{7,5},{8,6},{9,7},{10,... | collective-permute-start | bytes 1572872 | tf_op jit(solution)/shard_map/ppermute | solution.py:87
  33.7 0.9 fusion.1
  34.7 8.0 %collective-permute-done.1 = f32[256,512]{0,1:T(8,128)S(1)} collective-permute-done((f32[256,512]{0,1:T(8,128)}, f32[256,512]{0,1:T(8,128)S(1)}, u32[]{:S(2)}, u32[]{:S(2)}) %collective-permute-start.1) | collective-permute-done | bytes 524320 | tf_op jit(solution)/shard_map/ppermute | solution.py:86
  42.7 1.9 collective-permute-start.2
  44.6 0.0 collective-permute-done.5
  44.6 4.6 %collective-permute-start.6 = (f32[256,512]{0,1:T(8,128)S(1)}, f32[256,512]{0,1:T(8,128)S(1)}, u32[]{:S(2)}, u32[]{:S(2)}) collective-permute-start(f32[256,512]{0,1:T(8,128)S(1)} %collective-permute-done.5), channel_id=1, source_target_pairs={{0,14},{1,15},{2,0},{3,1},{4,2},{5,3},{6,4},{7,5},{8,6},{9,7},{10,... | collective-permute-start | bytes 1572872 | tf_op jit(solution)/shard_map/ppermute | solution.py:87
  49.2 4.6 %collective-permute-start.9 = (f32[256,512]{0,1:T(8,128)}, f32[256,512]{0,1:T(8,128)S(1)}, u32[]{:S(2)}, u32[]{:S(2)}) collective-permute-start(f32[256,512]{0,1:T(8,128)} %collective-permute-done), channel_id=1, source_target_pairs={{0,1},{1,0},{2,3},{3,2},{4,5},{5,4},{6,7},{7,6},{8,9},{9,8},{10,11... | collective-permute-start | bytes 1572872 | tf_op jit(solution)/shard_map/ppermute | solution.py:94
  53.8 1.9 %collective-permute-start.15 = (f32[256,512]{0,1:T(8,128)}, f32[256,512]{0,1:T(8,128)S(1)}, u32[]{:S(2)}, u32[]{:S(2)}) collective-permute-start(f32[256,512]{0,1:T(8,128)} %collective-permute-done.4), channel_id=1, source_target_pairs={{0,1},{1,0},{2,3},{3,2},{4,5},{5,4},{6,7},{7,6},{8,9},{9,8},{10,11... | collective-permute-start | bytes 1572872 | tf_op jit(solution)/shard_map/ppermute | solution.py:94
  55.7 1.9 bitcast_dynamic-update-slice_fusion.14
  57.6 1.9 %collective-permute-start.3 = (f32[128,512]{0,1:T(8,128)S(1)}, f32[128,512]{0,1:T(8,128)S(1)}, u32[]{:S(2)}, u32[]{:S(2)}) collective-permute-start(f32[128,512]{0,1:T(8,128)S(1)} %slice.66), channel_id=1, source_target_pairs={{0,2},{1,3},{2,4},{3,5},{4,6},{5,7},{6,8},{7,9},{8,10},{9,11},{10,... | collective-permute-start | bytes 786440 | tf_op jit(solution)/shard_map/ppermute | solution.py:91
  59.6 0.8 bitcast_dynamic-update-slice_fusion.13
  60.4 4.6 %collective-permute-start.7 = (f32[128,512]{0,1:T(8,128)S(1)}, f32[128,512]{0,1:T(8,128)S(1)}, u32[]{:S(2)}, u32[]{:S(2)}) collective-permute-start(f32[128,512]{0,1:T(8,128)S(1)} %slice.67), channel_id=1, source_target_pairs={{0,14},{1,15},{2,0},{3,1},{4,2},{5,3},{6,4},{7,5},{8,6},{9,7},{10,... | collective-permute-start | bytes 786440 | tf_op jit(solution)/shard_map/ppermute | solution.py:92
  65.0 0.8 bitcast_dynamic-update-slice_fusion.12
  65.8 0.1 collective-permute-done.3
  66.0 5.5 %collective-permute-start.10 = (f32[256,512]{0,1:T(8,128)S(1)}, f32[256,512]{0,1:T(8,128)S(1)}, u32[]{:S(2)}, u32[]{:S(2)}) collective-permute-start(f32[256,512]{0,1:T(8,128)S(1)} %collective-permute-done.1), channel_id=1, source_target_pairs={{0,1},{1,0},{2,3},{3,2},{4,5},{5,4},{6,7},{7,6},{8,9},{9,8},{10,11... | collective-permute-start | bytes 1572872 | tf_op jit(solution)/shard_map/ppermute | solution.py:94
  71.5 2.3 %collective-permute-start.14 = (f32[256,512]{0,1:T(8,128)S(1)}, f32[256,512]{0,1:T(8,128)S(1)}, u32[]{:S(2)}, u32[]{:S(2)}) collective-permute-start(f32[256,512]{0,1:T(8,128)S(1)} %collective-permute-done.5), channel_id=1, source_target_pairs={{0,1},{1,0},{2,3},{3,2},{4,5},{5,4},{6,7},{7,6},{8,9},{9,8},{10,11... | collective-permute-start | bytes 1572872 | tf_op jit(solution)/shard_map/ppermute | solution.py:94
  73.9 0.8 bitcast_dynamic-update-slice_fusion.11
  74.7 0.8 bitcast_dynamic-update-slice_fusion.10
  75.5 0.8 bitcast_dynamic-update-slice_fusion.9
  76.4 1.9 bitcast_dynamic-update-slice_fusion.8
  78.2 2.0 %collective-permute-start.11 = (f32[256,512]{0,1:T(8,128)S(1)}, f32[256,512]{0,1:T(8,128)S(1)}, u32[]{:S(2)}, u32[]{:S(2)}) collective-permute-start(f32[256,512]{0,1:T(8,128)S(1)} %collective-permute-done.2), channel_id=1, source_target_pairs={{0,1},{1,0},{2,3},{3,2},{4,5},{5,4},{6,7},{7,6},{8,9},{9,8},{10,11... | collective-permute-start | bytes 1572872 | tf_op jit(solution)/shard_map/ppermute | solution.py:94
  80.3 1.9 bitcast_dynamic-update-slice_fusion.7
  82.2 2.3 %collective-permute-start.12 = (f32[256,512]{0,1:T(8,128)S(1)}, f32[256,512]{0,1:T(8,128)S(1)}, u32[]{:S(2)}, u32[]{:S(2)}) collective-permute-start(f32[256,512]{0,1:T(8,128)S(1)} %constant_dynamic-update-slice_fusion), channel_id=1, source_target_pairs={{0,1},{1,0},{2,3},{3,2},{4,5},{5,4},{6,7},{7,6},{8,9},{9,8},{10,11... | collective-permute-start | bytes 1572872 | tf_op jit(solution)/shard_map/ppermute | solution.py:94
  84.4 0.8 bitcast_dynamic-update-slice_fusion.6
  85.3 2.0 %collective-permute-start.13 = (f32[256,512]{0,1:T(8,128)S(1)}, f32[256,512]{0,1:T(8,128)S(1)}, u32[]{:S(2)}, u32[]{:S(2)}) collective-permute-start(f32[256,512]{0,1:T(8,128)S(1)} %collective-permute-done.6), channel_id=1, source_target_pairs={{0,1},{1,0},{2,3},{3,2},{4,5},{5,4},{6,7},{7,6},{8,9},{9,8},{10,11... | collective-permute-start | bytes 1572872 | tf_op jit(solution)/shard_map/ppermute | solution.py:94
  87.3 0.8 bitcast_dynamic-update-slice_fusion.5
  88.2 0.8 bitcast_dynamic-update-slice_fusion.4
  89.0 0.8 bitcast_dynamic-update-slice_fusion.3
  89.9 0.8 bitcast_dynamic-update-slice_fusion.2
  90.7 0.8 bitcast_dynamic-update-slice_fusion.1
  91.5 0.9 bitcast_dynamic-update-slice_fusion
  92.4 7.7 %gather_fusion.1 = f32[16,256,512]{1,2,0:T(8,128)} fusion(f32[16,256,512]{1,2,0:T(8,128)} %bitcast_dynamic-update-slice_fusion, s32[1024]{0:T(1024)S(1)} %pad_clamp_fusion.2), kind=kCustom, calls=%fused_computation.3 | custom fusion | bytes 16777280 | tf_op jit(solution)/shard_map/jit(_take)/gather | solution.py:102
  100.1 4.2 %broadcast_select_fusion = f32[16,256,512]{1,2,0:T(8,128)S(1)} fusion(f32[16,256,512]{1,2,0:T(8,128)} %gather_fusion.1, pred[16]{0:T(512)(128)(4,1)S(1)} %compare_and_fusion.2), kind=kLoop, calls=%fused_computation.4 | loop fusion | flops 2097152 | bytes 16777232 | tf_op jit(solution)/shard_map/jit(_take)/select_n | solution.py:102
  104.4 0.1 fusion.15
  104.5 3.0 %fusion.14 = (f32[6,256,512]{1,2,0:T(8,128)}, f32[6,256,512]{1,2,0:T(8,128)}) fusion(f32[16,256,512]{1,2,0:T(8,128)S(1)} %broadcast_select_fusion), kind=kLoop, calls=%fused_computation.70 | loop fusion | bytes 12582912 | tf_op jit(solution)/shard_map/slice | solution.py:128
  107.5 0.3 copy.12
  107.8 0.3 copy.13
  108.2 1.8 gather_fusion.2
  110.0 1.6 gather_fusion.3
  111.6 3.1 %fusion.13.a_ref = f32[512,512]{1,0:T(8,128)} fusion(f32[512,512]{1,0:T(8,128)S(1)} %gather_fusion.3, f32[512,512]{1,0:T(8,128)S(1)} %gather_fusion.2, pred[512]{0:T(512)(128)(4,1)S(1)} %get-tuple-element.22, pred[512]{0:T(512)(128)(4,1)S(1)} %get-tuple-element.23), kind=kOutput, calls=%fused_computation.69 | convolution fusion | flops 1611399168 | bytes 3146752 | tf_op jit(solution)/shard_map/dot_general | solution.py:126
  114.7 59.1 %shard_map.28 = f32[512,512]{1,0:T(8,128)} custom-call(f32[512,512]{1,0:T(8,128)} %fusion.13.a_ref), custom_call_target="tpu_custom_call" | custom-call | flops 1610612736 | bytes 2097152 | tf_op jit(solution)/shard_map/pallas_call | solution.py:53
  173.9 4.2 %fusion.12 = f32[512,512]{1,0:T(8,128)} fusion(f32[512,512]{1,0:T(8,128)} %shard_map.28, f32[512,512]{1,0:T(8,128)S(1)} %gather_fusion.3, f32[512,512]{1,0:T(8,128)S(1)} %gather_fusion.2, pred[512]{0:T(512)(128)(4,1)S(1)} %get-tuple-element.22, pred[512]{0:T(512)(128)(4,1)S(1)} %get-tuple-element.23), kind=kOutput, calls=%fused_computation.68 | convolution fusion | flops 1611399168 | bytes 4195328 | tf_op jit(solution)/shard_map/dot_general | solution.py:127
  178.1 2.4 %copy.14 = f32[6,256,512]{2,1,0:T(8,128)S(1)} copy(f32[6,256,512]{1,2,0:T(8,128)} %get-tuple-element.8) | data formatting | bytes 6291456 | tf_op jit(solution)/shard_map/slice | solution.py:128
  180.5 3.6 %copy.15 = f32[6,256,512]{2,1,0:T(8,128)} copy(f32[6,256,512]{1,2,0:T(8,128)} %get-tuple-element.9) | data formatting | bytes 6291456 | tf_op jit(solution)/shard_map/slice | solution.py:129
  184.1 2.7 %fusion.2 = f32[256,512]{1,0:T(8,128)S(1)} fusion(f32[512,512]{1,0:T(8,128)} %fusion.12, f32[256,512]{0,1:T(8,128)} %copy-done.4, s32[256]{0:T(256)S(1)} %fusion.9, s32[512]{0:T(512)S(1)} %bitcast.71, pred[256]{0:T(512)(128)(4,1)S(1)} %get-tuple-element.20), kind=kOutput, calls=%fused_computation.30 | convolution fusion | flops 805699584 | bytes 2100480 | tf_op jit(solution)/shard_map/dot_general | solution.py:139
  186.8 1.5 convolution_bitcast_fusion.1
  188.3 1.6 convolution_bitcast_fusion
  190.0 1.5 fusion
  (38 shorter events, 0.2 us)
Async XLA Ops:
  0.0 21.1 %copy-start.3 = (f32[1,256,2048]{2,1,0:T(8,128)S(1)}, f32[1,256,2048]{2,1,0:T(8,128)}, u32[]{:S(2)}) copy-start(f32[1,256,2048]{2,1,0:T(8,128)} %param.4) | copy-start | bytes 6291460
  3.9 81.4 %copy-start.4 = (f32[256,512]{0,1:T(8,128)}, f32[256,512]{0,1:T(8,128)S(1)}, u32[]{:S(2)}) copy-start(f32[256,512]{0,1:T(8,128)S(1)} %bitcast_select_fusion.1) | copy-start | bytes 1572868
  3.9 23.2 %collective-permute-start = (f32[256,512]{0,1:T(8,128)S(1)}, f32[256,512]{0,1:T(8,128)}, u32[]{:S(2)}, u32[]{:S(2)}) collective-permute-start(f32[256,512]{0,1:T(8,128)S(1)} %bitcast_select_fusion.1), channel_id=1, source_target_pairs={{0,2},{1,3},{2,4},{3,5},{4,6},{5,7},{6,8},{7,9},{8,10},{9,11},{10,... | collective-permute-start | bytes 1572872 | tf_op jit(solution)/shard_map/ppermute | solution.py:86
  8.7 20.4 %collective-permute-start.4 = (f32[256,512]{0,1:T(8,128)S(1)}, f32[256,512]{0,1:T(8,128)}, u32[]{:S(2)}, u32[]{:S(2)}) collective-permute-start(f32[256,512]{0,1:T(8,128)S(1)} %bitcast_select_fusion.1), channel_id=1, source_target_pairs={{0,14},{1,15},{2,0},{3,1},{4,2},{5,3},{6,4},{7,5},{8,6},{9,7},{10,... | collective-permute-start | bytes 1572872 | tf_op jit(solution)/shard_map/ppermute | solution.py:87
  17.3 60.9 %collective-permute-start.8 = (f32[256,512]{0,1:T(8,128)S(1)}, f32[256,512]{0,1:T(8,128)}, u32[]{:S(2)}, u32[]{:S(2)}) collective-permute-start(f32[256,512]{0,1:T(8,128)S(1)} %bitcast_select_fusion.1), channel_id=1, source_target_pairs={{0,1},{1,0},{2,3},{3,2},{4,5},{5,4},{6,7},{7,6},{8,9},{9,8},{10,11... | collective-permute-start | bytes 1572872 | tf_op jit(solution)/shard_map/ppermute | solution.py:94
  27.1 15.5 %collective-permute-start.1 = (f32[256,512]{0,1:T(8,128)}, f32[256,512]{0,1:T(8,128)S(1)}, u32[]{:S(2)}, u32[]{:S(2)}) collective-permute-start(f32[256,512]{0,1:T(8,128)} %collective-permute-done), channel_id=1, source_target_pairs={{0,2},{1,3},{2,4},{3,5},{4,6},{5,7},{6,8},{7,9},{8,10},{9,11},{10,... | collective-permute-start | bytes 1572872 | tf_op jit(solution)/shard_map/ppermute | solution.py:86
  29.1 15.5 %collective-permute-start.5 = (f32[256,512]{0,1:T(8,128)}, f32[256,512]{0,1:T(8,128)S(1)}, u32[]{:S(2)}, u32[]{:S(2)}) collective-permute-start(f32[256,512]{0,1:T(8,128)} %collective-permute-done.4), channel_id=1, source_target_pairs={{0,14},{1,15},{2,0},{3,1},{4,2},{5,3},{6,4},{7,5},{8,6},{9,7},{10,... | collective-permute-start | bytes 1572872 | tf_op jit(solution)/shard_map/ppermute | solution.py:87
  42.7 15.0 %collective-permute-start.2 = (f32[256,512]{0,1:T(8,128)S(1)}, f32[256,512]{0,1:T(8,128)S(1)}, u32[]{:S(2)}, u32[]{:S(2)}) collective-permute-start(f32[256,512]{0,1:T(8,128)S(1)} %collective-permute-done.1), channel_id=1, source_target_pairs={{0,2},{1,3},{2,4},{3,5},{4,6},{5,7},{6,8},{7,9},{8,10},{9,11},{10,... | collective-permute-start | bytes 1572872 | tf_op jit(solution)/shard_map/ppermute | solution.py:86
  44.6 15.8 %collective-permute-start.6 = (f32[256,512]{0,1:T(8,128)S(1)}, f32[256,512]{0,1:T(8,128)S(1)}, u32[]{:S(2)}, u32[]{:S(2)}) collective-permute-start(f32[256,512]{0,1:T(8,128)S(1)} %collective-permute-done.5), channel_id=1, source_target_pairs={{0,14},{1,15},{2,0},{3,1},{4,2},{5,3},{6,4},{7,5},{8,6},{9,7},{10,... | collective-permute-start | bytes 1572872 | tf_op jit(solution)/shard_map/ppermute | solution.py:87
  49.2 32.9 %collective-permute-start.9 = (f32[256,512]{0,1:T(8,128)}, f32[256,512]{0,1:T(8,128)S(1)}, u32[]{:S(2)}, u32[]{:S(2)}) collective-permute-start(f32[256,512]{0,1:T(8,128)} %collective-permute-done), channel_id=1, source_target_pairs={{0,1},{1,0},{2,3},{3,2},{4,5},{5,4},{6,7},{7,6},{8,9},{9,8},{10,11... | collective-permute-start | bytes 1572872 | tf_op jit(solution)/shard_map/ppermute | solution.py:94
  53.8 37.7 %collective-permute-start.15 = (f32[256,512]{0,1:T(8,128)}, f32[256,512]{0,1:T(8,128)S(1)}, u32[]{:S(2)}, u32[]{:S(2)}) collective-permute-start(f32[256,512]{0,1:T(8,128)} %collective-permute-done.4), channel_id=1, source_target_pairs={{0,1},{1,0},{2,3},{3,2},{4,5},{5,4},{6,7},{7,6},{8,9},{9,8},{10,11... | collective-permute-start | bytes 1572872 | tf_op jit(solution)/shard_map/ppermute | solution.py:94
  57.6 8.3 %collective-permute-start.3 = (f32[128,512]{0,1:T(8,128)S(1)}, f32[128,512]{0,1:T(8,128)S(1)}, u32[]{:S(2)}, u32[]{:S(2)}) collective-permute-start(f32[128,512]{0,1:T(8,128)S(1)} %slice.66), channel_id=1, source_target_pairs={{0,2},{1,3},{2,4},{3,5},{4,6},{5,7},{6,8},{7,9},{8,10},{9,11},{10,... | collective-permute-start | bytes 786440 | tf_op jit(solution)/shard_map/ppermute | solution.py:91
  60.4 11.1 %collective-permute-start.7 = (f32[128,512]{0,1:T(8,128)S(1)}, f32[128,512]{0,1:T(8,128)S(1)}, u32[]{:S(2)}, u32[]{:S(2)}) collective-permute-start(f32[128,512]{0,1:T(8,128)S(1)} %slice.67), channel_id=1, source_target_pairs={{0,14},{1,15},{2,0},{3,1},{4,2},{5,3},{6,4},{7,5},{8,6},{9,7},{10,... | collective-permute-start | bytes 786440 | tf_op jit(solution)/shard_map/ppermute | solution.py:92
  66.0 19.3 %collective-permute-start.10 = (f32[256,512]{0,1:T(8,128)S(1)}, f32[256,512]{0,1:T(8,128)S(1)}, u32[]{:S(2)}, u32[]{:S(2)}) collective-permute-start(f32[256,512]{0,1:T(8,128)S(1)} %collective-permute-done.1), channel_id=1, source_target_pairs={{0,1},{1,0},{2,3},{3,2},{4,5},{5,4},{6,7},{7,6},{8,9},{9,8},{10,11... | collective-permute-start | bytes 1572872 | tf_op jit(solution)/shard_map/ppermute | solution.py:94
  71.5 19.2 %collective-permute-start.14 = (f32[256,512]{0,1:T(8,128)S(1)}, f32[256,512]{0,1:T(8,128)S(1)}, u32[]{:S(2)}, u32[]{:S(2)}) collective-permute-start(f32[256,512]{0,1:T(8,128)S(1)} %collective-permute-done.5), channel_id=1, source_target_pairs={{0,1},{1,0},{2,3},{3,2},{4,5},{5,4},{6,7},{7,6},{8,9},{9,8},{10,11... | collective-permute-start | bytes 1572872 | tf_op jit(solution)/shard_map/ppermute | solution.py:94
  78.2 9.9 %collective-permute-start.11 = (f32[256,512]{0,1:T(8,128)S(1)}, f32[256,512]{0,1:T(8,128)S(1)}, u32[]{:S(2)}, u32[]{:S(2)}) collective-permute-start(f32[256,512]{0,1:T(8,128)S(1)} %collective-permute-done.2), channel_id=1, source_target_pairs={{0,1},{1,0},{2,3},{3,2},{4,5},{5,4},{6,7},{7,6},{8,9},{9,8},{10,11... | collective-permute-start | bytes 1572872 | tf_op jit(solution)/shard_map/ppermute | solution.py:94
  82.2 6.9 %collective-permute-start.12 = (f32[256,512]{0,1:T(8,128)S(1)}, f32[256,512]{0,1:T(8,128)S(1)}, u32[]{:S(2)}, u32[]{:S(2)}) collective-permute-start(f32[256,512]{0,1:T(8,128)S(1)} %constant_dynamic-update-slice_fusion), channel_id=1, source_target_pairs={{0,1},{1,0},{2,3},{3,2},{4,5},{5,4},{6,7},{7,6},{8,9},{9,8},{10,11... | collective-permute-start | bytes 1572872 | tf_op jit(solution)/shard_map/ppermute | solution.py:94
  85.3 4.6 %collective-permute-start.13 = (f32[256,512]{0,1:T(8,128)S(1)}, f32[256,512]{0,1:T(8,128)S(1)}, u32[]{:S(2)}, u32[]{:S(2)}) collective-permute-start(f32[256,512]{0,1:T(8,128)S(1)} %collective-permute-done.6), channel_id=1, source_target_pairs={{0,1},{1,0},{2,3},{3,2},{4,5},{5,4},{6,7},{7,6},{8,9},{9,8},{10,11... | collective-permute-start | bytes 1572872 | tf_op jit(solution)/shard_map/ppermute | solution.py:94
  184.1 4.2 %copy-start = (f32[6,256,512]{2,1,0:T(8,128)S(1)}, f32[6,256,512]{2,1,0:T(8,128)}, u32[]{:S(2)}) copy-start(f32[6,256,512]{2,1,0:T(8,128)} %copy.15) | copy-start | bytes 9437188
  184.1 5.9 %copy-start.1 = (f32[1,256,1536]{2,1,0:T(8,128)S(1)}, f32[1,256,1536]{2,1,0:T(8,128)}, u32[]{:S(2)}) copy-start(f32[1,256,1536]{2,1,0:T(8,128)} %get-tuple-element.12) | copy-start | bytes 4718596
  184.1 5.9 %copy-start.2 = (f32[1,256,1536]{2,1,0:T(8,128)S(1)}, f32[1,256,1536]{2,1,0:T(8,128)}, u32[]{:S(2)}) copy-start(f32[1,256,1536]{2,1,0:T(8,128)} %get-tuple-element.13) | copy-start | bytes 4718596

commit v5 on v4

--- a/solution.py
+++ b/solution.py
@@ -124,7 +124,7 @@
     g_b = full[chips // 2 :].reshape(width, inner)
     schur = jnp.take(g_a[outer:], index_a, axis=0) + jnp.take(g_b[outer:], index_b, axis=0)
     squared = jnp.dot(schur, schur, precision=HI)
-    sinv = jnp.dot(spd_inverse(squared), schur, precision=HI)
+    sinv = jnp.dot(spd_inverse(squared), schur, precision=lax.Precision.HIGH)
     first_ext = g_a[:outer]
     second_ext = g_b[:outer]
     global_rows = lax.axis_index("row") * rows_here + jnp.arange(rows_here, dtype=jnp.int32)
@@ -136,7 +136,7 @@
     left_part = jnp.where(jnp.logical_and(is_first, global_rows < outer)[:, None], local_ext, zero)
     right_part = jnp.where(is_first, zero, local_ext)
     base = jnp.concatenate([left_part, right_part], 1)
-    solved = jnp.dot(left, sinv, precision=HI)
+    solved = jnp.dot(left, sinv, precision=lax.Precision.HIGH)
     contract = (((1,), (1,)), ((), ()))
     update_first = lax.dot_general(solved, first_ext, contract, precision=lax.Precision.HIGH)
     update_second = lax.dot_general(solved, second_ext, contract, precision=lax.Precision.HIGH)

time: 192 us -> 191 us (level)
  no operation moved by 1% of the time
where the time goes in v5:
time: 191 us; the launch traced here: 190 us
  Pallas kernels  59.1 us (31%)
  starting transfers between devices  56.6 us (30%)
  local copies, waits for them, and re-layouts  40.4 us (21%)
  waiting for transfers between devices  12.1 us (6%)
  matrix products  11.9 us (6%)
  other arithmetic  9.67 us (5%)
    pallas_call x1, Pallas kernels, spd_inverse(): pl.pallas_call(_gj_kernel, out_shape=jax.ShapeDtypeStruct((n, n), jnp.flo...  59.1 us
    ppermute x8, starting transfers between devices, ring_gather(): sib = [lax.ppermute(piece, AXES, swap) for piece in rel]  23.7 us
    ppermute x3, starting transfers between devices, ring_gather(): b = lax.ppermute(b, AXES, ccw)  17.7 us
    unnamed x25, local copies, waits for them, and re-layouts  14.9 us
    ppermute x3, waiting for transfers between devices, ring_gather(): a = lax.ppermute(a, AXES, cw)  11.9 us
    ppermute x3, starting transfers between devices, ring_gather(): a = lax.ppermute(a, AXES, cw)  8.64 us
    gather x1, local copies, waits for them, and re-layouts, ring_gather(): full = jnp.take(stacked, idx, axis=0)  7.69 us
    slice x2, local copies, waits for them, and re-layouts, body(): first_ext = g_a[:outer]  5.36 us
  transfers between devices with their start and end apart: 16, of which 3 were waited for; matrix products, arithmetic and copies ran while one was open for 10% of the time, Pallas kernels for 0%

profile of v5, /device:TPU:1, one launch (start us, length us, event | category | flops | bytes accessed | tf_op | source)
XLA Modules:
  0.0 190.2 jit_solution(939364047902403305)
XLA Ops:
  0.0 0.9 compare_select_fusion
  0.9 1.1 slice.65
  2.0 0.2 copy.9
  2.2 1.6 gather_fusion
  3.8 0.1 bitcast_select_fusion.1
  3.9 4.8 %collective-permute-start = (f32[256,512]{0,1:T(8,128)S(1)}, f32[256,512]{0,1:T(8,128)}, u32[]{:S(2)}, u32[]{:S(2)}) collective-permute-start(f32[256,512]{0,1:T(8,128)S(1)} %bitcast_select_fusion.1), channel_id=1, source_target_pairs={{0,2},{1,3},{2,4},{3,5},{4,6},{5,7},{6,8},{7,9},{8,10},{9,11},{10,... | collective-permute-start | bytes 1572872 | tf_op jit(solution)/shard_map/ppermute | solution.py:86
  8.7 8.6 %collective-permute-start.4 = (f32[256,512]{0,1:T(8,128)S(1)}, f32[256,512]{0,1:T(8,128)}, u32[]{:S(2)}, u32[]{:S(2)}) collective-permute-start(f32[256,512]{0,1:T(8,128)S(1)} %bitcast_select_fusion.1), channel_id=1, source_target_pairs={{0,14},{1,15},{2,0},{3,1},{4,2},{5,3},{6,4},{7,5},{8,6},{9,7},{10,... | collective-permute-start | bytes 1572872 | tf_op jit(solution)/shard_map/ppermute | solution.py:87
  17.3 2.9 %collective-permute-start.8 = (f32[256,512]{0,1:T(8,128)S(1)}, f32[256,512]{0,1:T(8,128)}, u32[]{:S(2)}, u32[]{:S(2)}) collective-permute-start(f32[256,512]{0,1:T(8,128)S(1)} %bitcast_select_fusion.1), channel_id=1, source_target_pairs={{0,1},{1,0},{2,3},{3,2},{4,5},{5,4},{6,7},{7,6},{8,9},{9,8},{10,11... | collective-permute-start | bytes 1572872 | tf_op jit(solution)/shard_map/ppermute | solution.py:94
  20.3 0.8 constant_dynamic-slice_fusion.1
  21.1 1.9 select_bitcast_fusion.1
  23.0 0.1 copy.10
  23.1 0.1 reshape.235
  23.2 3.9 %collective-permute-done = f32[256,512]{0,1:T(8,128)} collective-permute-done((f32[256,512]{0,1:T(8,128)S(1)}, f32[256,512]{0,1:T(8,128)}, u32[]{:S(2)}, u32[]{:S(2)}) %collective-permute-start) | collective-permute-done | bytes 524320 | tf_op jit(solution)/shard_map/ppermute | solution.py:86
  27.1 1.9 %collective-permute-start.1 = (f32[256,512]{0,1:T(8,128)}, f32[256,512]{0,1:T(8,128)S(1)}, u32[]{:S(2)}, u32[]{:S(2)}) collective-permute-start(f32[256,512]{0,1:T(8,128)} %collective-permute-done), channel_id=1, source_target_pairs={{0,2},{1,3},{2,4},{3,5},{4,6},{5,7},{6,8},{7,9},{8,10},{9,11},{10,... | collective-permute-start | bytes 1572872 | tf_op jit(solution)/shard_map/ppermute | solution.py:86
  29.1 0.1 reshape.234
  29.1 0.0 collective-permute-done.4
  29.1 4.6 %collective-permute-start.5 = (f32[256,512]{0,1:T(8,128)}, f32[256,512]{0,1:T(8,128)S(1)}, u32[]{:S(2)}, u32[]{:S(2)}) collective-permute-start(f32[256,512]{0,1:T(8,128)} %collective-permute-done.4), channel_id=1, source_target_pairs={{0,14},{1,15},{2,0},{3,1},{4,2},{5,3},{6,4},{7,5},{8,6},{9,7},{10,... | collective-permute-start | bytes 1572872 | tf_op jit(solution)/shard_map/ppermute | solution.py:87
  33.7 0.9 fusion.1
  34.7 8.0 %collective-permute-done.1 = f32[256,512]{0,1:T(8,128)S(1)} collective-permute-done((f32[256,512]{0,1:T(8,128)}, f32[256,512]{0,1:T(8,128)S(1)}, u32[]{:S(2)}, u32[]{:S(2)}) %collective-permute-start.1) | collective-permute-done | bytes 524320 | tf_op jit(solution)/shard_map/ppermute | solution.py:86
  42.7 1.9 %collective-permute-start.2 = (f32[256,512]{0,1:T(8,128)S(1)}, f32[256,512]{0,1:T(8,128)S(1)}, u32[]{:S(2)}, u32[]{:S(2)}) collective-permute-start(f32[256,512]{0,1:T(8,128)S(1)} %collective-permute-done.1), channel_id=1, source_target_pairs={{0,2},{1,3},{2,4},{3,5},{4,6},{5,7},{6,8},{7,9},{8,10},{9,11},{10,... | collective-permute-start | bytes 1572872 | tf_op jit(solution)/shard_map/ppermute | solution.py:86
  44.6 0.0 collective-permute-done.5
  44.6 4.6 %collective-permute-start.6 = (f32[256,512]{0,1:T(8,128)S(1)}, f32[256,512]{0,1:T(8,128)S(1)}, u32[]{:S(2)}, u32[]{:S(2)}) collective-permute-start(f32[256,512]{0,1:T(8,128)S(1)} %collective-permute-done.5), channel_id=1, source_target_pairs={{0,14},{1,15},{2,0},{3,1},{4,2},{5,3},{6,4},{7,5},{8,6},{9,7},{10,... | collective-permute-start | bytes 1572872 | tf_op jit(solution)/shard_map/ppermute | solution.py:87
  49.2 4.6 %collective-permute-start.9 = (f32[256,512]{0,1:T(8,128)}, f32[256,512]{0,1:T(8,128)S(1)}, u32[]{:S(2)}, u32[]{:S(2)}) collective-permute-start(f32[256,512]{0,1:T(8,128)} %collective-permute-done), channel_id=1, source_target_pairs={{0,1},{1,0},{2,3},{3,2},{4,5},{5,4},{6,7},{7,6},{8,9},{9,8},{10,11... | collective-permute-start | bytes 1572872 | tf_op jit(solution)/shard_map/ppermute | solution.py:94
  53.8 1.9 %collective-permute-start.15 = (f32[256,512]{0,1:T(8,128)}, f32[256,512]{0,1:T(8,128)S(1)}, u32[]{:S(2)}, u32[]{:S(2)}) collective-permute-start(f32[256,512]{0,1:T(8,128)} %collective-permute-done.4), channel_id=1, source_target_pairs={{0,1},{1,0},{2,3},{3,2},{4,5},{5,4},{6,7},{7,6},{8,9},{9,8},{10,11... | collective-permute-start | bytes 1572872 | tf_op jit(solution)/shard_map/ppermute | solution.py:94
  55.7 1.9 bitcast_dynamic-update-slice_fusion.14
  57.6 1.9 %collective-permute-start.3 = (f32[128,512]{0,1:T(8,128)S(1)}, f32[128,512]{0,1:T(8,128)S(1)}, u32[]{:S(2)}, u32[]{:S(2)}) collective-permute-start(f32[128,512]{0,1:T(8,128)S(1)} %slice.66), channel_id=1, source_target_pairs={{0,2},{1,3},{2,4},{3,5},{4,6},{5,7},{6,8},{7,9},{8,10},{9,11},{10,... | collective-permute-start | bytes 786440 | tf_op jit(solution)/shard_map/ppermute | solution.py:91
  59.6 0.8 bitcast_dynamic-update-slice_fusion.13
  60.4 4.6 %collective-permute-start.7 = (f32[128,512]{0,1:T(8,128)S(1)}, f32[128,512]{0,1:T(8,128)S(1)}, u32[]{:S(2)}, u32[]{:S(2)}) collective-permute-start(f32[128,512]{0,1:T(8,128)S(1)} %slice.67), channel_id=1, source_target_pairs={{0,14},{1,15},{2,0},{3,1},{4,2},{5,3},{6,4},{7,5},{8,6},{9,7},{10,... | collective-permute-start | bytes 786440 | tf_op jit(solution)/shard_map/ppermute | solution.py:92
  65.0 0.8 bitcast_dynamic-update-slice_fusion.12
  65.8 0.1 collective-permute-done.3
  66.0 5.5 %collective-permute-start.10 = (f32[256,512]{0,1:T(8,128)S(1)}, f32[256,512]{0,1:T(8,128)S(1)}, u32[]{:S(2)}, u32[]{:S(2)}) collective-permute-start(f32[256,512]{0,1:T(8,128)S(1)} %collective-permute-done.1), channel_id=1, source_target_pairs={{0,1},{1,0},{2,3},{3,2},{4,5},{5,4},{6,7},{7,6},{8,9},{9,8},{10,11... | collective-permute-start | bytes 1572872 | tf_op jit(solution)/shard_map/ppermute | solution.py:94
  71.5 2.3 %collective-permute-start.14 = (f32[256,512]{0,1:T(8,128)S(1)}, f32[256,512]{0,1:T(8,128)S(1)}, u32[]{:S(2)}, u32[]{:S(2)}) collective-permute-start(f32[256,512]{0,1:T(8,128)S(1)} %collective-permute-done.5), channel_id=1, source_target_pairs={{0,1},{1,0},{2,3},{3,2},{4,5},{5,4},{6,7},{7,6},{8,9},{9,8},{10,11... | collective-permute-start | bytes 1572872 | tf_op jit(solution)/shard_map/ppermute | solution.py:94
  73.9 0.8 bitcast_dynamic-update-slice_fusion.11
  74.7 0.8 bitcast_dynamic-update-slice_fusion.10
  75.5 0.8 bitcast_dynamic-update-slice_fusion.9
  76.4 1.9 bitcast_dynamic-update-slice_fusion.8
  78.2 2.0 %collective-permute-start.11 = (f32[256,512]{0,1:T(8,128)S(1)}, f32[256,512]{0,1:T(8,128)S(1)}, u32[]{:S(2)}, u32[]{:S(2)}) collective-permute-start(f32[256,512]{0,1:T(8,128)S(1)} %collective-permute-done.2), channel_id=1, source_target_pairs={{0,1},{1,0},{2,3},{3,2},{4,5},{5,4},{6,7},{7,6},{8,9},{9,8},{10,11... | collective-permute-start | bytes 1572872 | tf_op jit(solution)/shard_map/ppermute | solution.py:94
  80.3 1.9 bitcast_dynamic-update-slice_fusion.7
  82.2 2.3 %collective-permute-start.12 = (f32[256,512]{0,1:T(8,128)S(1)}, f32[256,512]{0,1:T(8,128)S(1)}, u32[]{:S(2)}, u32[]{:S(2)}) collective-permute-start(f32[256,512]{0,1:T(8,128)S(1)} %constant_dynamic-update-slice_fusion), channel_id=1, source_target_pairs={{0,1},{1,0},{2,3},{3,2},{4,5},{5,4},{6,7},{7,6},{8,9},{9,8},{10,11... | collective-permute-start | bytes 1572872 | tf_op jit(solution)/shard_map/ppermute | solution.py:94
  84.4 0.8 bitcast_dynamic-update-slice_fusion.6
  85.3 2.2 %collective-permute-start.13 = (f32[256,512]{0,1:T(8,128)S(1)}, f32[256,512]{0,1:T(8,128)S(1)}, u32[]{:S(2)}, u32[]{:S(2)}) collective-permute-start(f32[256,512]{0,1:T(8,128)S(1)} %collective-permute-done.6), channel_id=1, source_target_pairs={{0,1},{1,0},{2,3},{3,2},{4,5},{5,4},{6,7},{7,6},{8,9},{9,8},{10,11... | collective-permute-start | bytes 1572872 | tf_op jit(solution)/shard_map/ppermute | solution.py:94
  87.5 0.8 bitcast_dynamic-update-slice_fusion.5
  88.4 0.8 bitcast_dynamic-update-slice_fusion.4
  89.2 0.8 bitcast_dynamic-update-slice_fusion.3
  90.0 0.8 bitcast_dynamic-update-slice_fusion.2
  90.9 0.8 bitcast_dynamic-update-slice_fusion.1
  91.7 0.9 bitcast_dynamic-update-slice_fusion
  92.6 7.7 %gather_fusion.1 = f32[16,256,512]{1,2,0:T(8,128)} fusion(f32[16,256,512]{1,2,0:T(8,128)} %bitcast_dynamic-update-slice_fusion, s32[1024]{0:T(1024)S(1)} %pad_clamp_fusion.2), kind=kCustom, calls=%fused_computation.3 | custom fusion | bytes 16777280 | tf_op jit(solution)/shard_map/jit(_take)/gather | solution.py:102
  100.3 4.2 %broadcast_select_fusion = f32[16,256,512]{1,2,0:T(8,128)S(1)} fusion(f32[16,256,512]{1,2,0:T(8,128)} %gather_fusion.1, pred[16]{0:T(512)(128)(4,1)S(1)} %compare_and_fusion.2), kind=kLoop, calls=%fused_computation.4 | loop fusion | flops 2097152 | bytes 16777232 | tf_op jit(solution)/shard_map/jit(_take)/select_n | solution.py:102
  104.6 0.1 fusion.15
  104.7 3.0 %fusion.14 = (f32[6,256,512]{1,2,0:T(8,128)}, f32[6,256,512]{1,2,0:T(8,128)}) fusion(f32[16,256,512]{1,2,0:T(8,128)S(1)} %broadcast_select_fusion), kind=kLoop, calls=%fused_computation.70 | loop fusion | bytes 12582912 | tf_op jit(solution)/shard_map/slice | solution.py:128
  107.7 0.3 copy.12
  108.0 0.3 copy.13
  108.4 1.6 gather_fusion.2
  110.0 1.6 gather_fusion.3
  111.6 3.1 %fusion.13.a_ref = f32[512,512]{1,0:T(8,128)} fusion(f32[512,512]{1,0:T(8,128)S(1)} %gather_fusion.3, f32[512,512]{1,0:T(8,128)S(1)} %gather_fusion.2, pred[512]{0:T(512)(128)(4,1)S(1)} %get-tuple-element.22, pred[512]{0:T(512)(128)(4,1)S(1)} %get-tuple-element.23), kind=kOutput, calls=%fused_computation.69 | convolution fusion | flops 1611399168 | bytes 3146752 | tf_op jit(solution)/shard_map/dot_general | solution.py:126
  114.7 59.1 %shard_map.28 = f32[512,512]{1,0:T(8,128)} custom-call(f32[512,512]{1,0:T(8,128)} %fusion.13.a_ref), custom_call_target="tpu_custom_call" | custom-call | flops 1610612736 | bytes 2097152 | tf_op jit(solution)/shard_map/pallas_call | solution.py:53
  173.9 3.3 %fusion.12 = f32[512,512]{1,0:T(8,128)} fusion(f32[512,512]{1,0:T(8,128)} %shard_map.28, f32[512,512]{1,0:T(8,128)S(1)} %gather_fusion.3, f32[512,512]{1,0:T(8,128)S(1)} %gather_fusion.2, pred[512]{0:T(512)(128)(4,1)S(1)} %get-tuple-element.22, pred[512]{0:T(512)(128)(4,1)S(1)} %get-tuple-element.23), kind=kOutput, calls=%fused_computation.68 | convolution fusion | flops 806092800 | bytes 4195328 | tf_op jit(solution)/shard_map/dot_general | solution.py:127
  177.2 2.4 %copy.14 = f32[6,256,512]{2,1,0:T(8,128)S(1)} copy(f32[6,256,512]{1,2,0:T(8,128)} %get-tuple-element.8) | data formatting | bytes 6291456 | tf_op jit(solution)/shard_map/slice | solution.py:128
  179.6 3.6 %copy.15 = f32[6,256,512]{2,1,0:T(8,128)} copy(f32[6,256,512]{1,2,0:T(8,128)} %get-tuple-element.9) | data formatting | bytes 6291456 | tf_op jit(solution)/shard_map/slice | solution.py:129
  183.2 2.2 %fusion.2 = f32[256,512]{1,0:T(8,128)S(1)} fusion(f32[512,512]{1,0:T(8,128)} %fusion.12, f32[256,512]{0,1:T(8,128)} %copy-done.4, s32[256]{0:T(256)S(1)} %fusion.9, s32[512]{0:T(512)S(1)} %bitcast.71, pred[256]{0:T(512)(128)(4,1)S(1)} %get-tuple-element.20), kind=kOutput, calls=%fused_computation.30 | convolution fusion | flops 403046400 | bytes 2100480 | tf_op jit(solution)/shard_map/dot_general | solution.py:139
  185.4 1.5 convolution_bitcast_fusion.1
  187.0 1.6 convolution_bitcast_fusion
  188.7 1.5 fusion
  (38 shorter events, 0.2 us)
Async XLA Ops:
  0.0 21.1 %copy-start.3 = (f32[1,256,2048]{2,1,0:T(8,128)S(1)}, f32[1,256,2048]{2,1,0:T(8,128)}, u32[]{:S(2)}) copy-start(f32[1,256,2048]{2,1,0:T(8,128)} %param.4) | copy-start | bytes 6291460
  3.9 81.4 %copy-start.4 = (f32[256,512]{0,1:T(8,128)}, f32[256,512]{0,1:T(8,128)S(1)}, u32[]{:S(2)}) copy-start(f32[256,512]{0,1:T(8,128)S(1)} %bitcast_select_fusion.1) | copy-start | bytes 1572868
  3.9 23.2 %collective-permute-start = (f32[256,512]{0,1:T(8,128)S(1)}, f32[256,512]{0,1:T(8,128)}, u32[]{:S(2)}, u32[]{:S(2)}) collective-permute-start(f32[256,512]{0,1:T(8,128)S(1)} %bitcast_select_fusion.1), channel_id=1, source_target_pairs={{0,2},{1,3},{2,4},{3,5},{4,6},{5,7},{6,8},{7,9},{8,10},{9,11},{10,... | collective-permute-start | bytes 1572872 | tf_op jit(solution)/shard_map/ppermute | solution.py:86
  8.7 20.4 %collective-permute-start.4 = (f32[256,512]{0,1:T(8,128)S(1)}, f32[256,512]{0,1:T(8,128)}, u32[]{:S(2)}, u32[]{:S(2)}) collective-permute-start(f32[256,512]{0,1:T(8,128)S(1)} %bitcast_select_fusion.1), channel_id=1, source_target_pairs={{0,14},{1,15},{2,0},{3,1},{4,2},{5,3},{6,4},{7,5},{8,6},{9,7},{10,... | collective-permute-start | bytes 1572872 | tf_op jit(solution)/shard_map/ppermute | solution.py:87
  17.3 60.9 %collective-permute-start.8 = (f32[256,512]{0,1:T(8,128)S(1)}, f32[256,512]{0,1:T(8,128)}, u32[]{:S(2)}, u32[]{:S(2)}) collective-permute-start(f32[256,512]{0,1:T(8,128)S(1)} %bitcast_select_fusion.1), channel_id=1, source_target_pairs={{0,1},{1,0},{2,3},{3,2},{4,5},{5,4},{6,7},{7,6},{8,9},{9,8},{10,11... | collective-permute-start | bytes 1572872 | tf_op jit(solution)/shard_map/ppermute | solution.py:94
  27.1 15.5 %collective-permute-start.1 = (f32[256,512]{0,1:T(8,128)}, f32[256,512]{0,1:T(8,128)S(1)}, u32[]{:S(2)}, u32[]{:S(2)}) collective-permute-start(f32[256,512]{0,1:T(8,128)} %collective-permute-done), channel_id=1, source_target_pairs={{0,2},{1,3},{2,4},{3,5},{4,6},{5,7},{6,8},{7,9},{8,10},{9,11},{10,... | collective-permute-start | bytes 1572872 | tf_op jit(solution)/shard_map/ppermute | solution.py:86
  29.1 15.5 %collective-permute-start.5 = (f32[256,512]{0,1:T(8,128)}, f32[256,512]{0,1:T(8,128)S(1)}, u32[]{:S(2)}, u32[]{:S(2)}) collective-permute-start(f32[256,512]{0,1:T(8,128)} %collective-permute-done.4), channel_id=1, source_target_pairs={{0,14},{1,15},{2,0},{3,1},{4,2},{5,3},{6,4},{7,5},{8,6},{9,7},{10,... | collective-permute-start | bytes 1572872 | tf_op jit(solution)/shard_map/ppermute | solution.py:87
  42.7 15.0 %collective-permute-start.2 = (f32[256,512]{0,1:T(8,128)S(1)}, f32[256,512]{0,1:T(8,128)S(1)}, u32[]{:S(2)}, u32[]{:S(2)}) collective-permute-start(f32[256,512]{0,1:T(8,128)S(1)} %collective-permute-done.1), channel_id=1, source_target_pairs={{0,2},{1,3},{2,4},{3,5},{4,6},{5,7},{6,8},{7,9},{8,10},{9,11},{10,... | collective-permute-start | bytes 1572872 | tf_op jit(solution)/shard_map/ppermute | solution.py:86
  44.6 15.8 %collective-permute-start.6 = (f32[256,512]{0,1:T(8,128)S(1)}, f32[256,512]{0,1:T(8,128)S(1)}, u32[]{:S(2)}, u32[]{:S(2)}) collective-permute-start(f32[256,512]{0,1:T(8,128)S(1)} %collective-permute-done.5), channel_id=1, source_target_pairs={{0,14},{1,15},{2,0},{3,1},{4,2},{5,3},{6,4},{7,5},{8,6},{9,7},{10,... | collective-permute-start | bytes 1572872 | tf_op jit(solution)/shard_map/ppermute | solution.py:87
  49.2 32.9 %collective-permute-start.9 = (f32[256,512]{0,1:T(8,128)}, f32[256,512]{0,1:T(8,128)S(1)}, u32[]{:S(2)}, u32[]{:S(2)}) collective-permute-start(f32[256,512]{0,1:T(8,128)} %collective-permute-done), channel_id=1, source_target_pairs={{0,1},{1,0},{2,3},{3,2},{4,5},{5,4},{6,7},{7,6},{8,9},{9,8},{10,11... | collective-permute-start | bytes 1572872 | tf_op jit(solution)/shard_map/ppermute | solution.py:94
  53.8 37.9 %collective-permute-start.15 = (f32[256,512]{0,1:T(8,128)}, f32[256,512]{0,1:T(8,128)S(1)}, u32[]{:S(2)}, u32[]{:S(2)}) collective-permute-start(f32[256,512]{0,1:T(8,128)} %collective-permute-done.4), channel_id=1, source_target_pairs={{0,1},{1,0},{2,3},{3,2},{4,5},{5,4},{6,7},{7,6},{8,9},{9,8},{10,11... | collective-permute-start | bytes 1572872 | tf_op jit(solution)/shard_map/ppermute | solution.py:94
  57.6 8.3 %collective-permute-start.3 = (f32[128,512]{0,1:T(8,128)S(1)}, f32[128,512]{0,1:T(8,128)S(1)}, u32[]{:S(2)}, u32[]{:S(2)}) collective-permute-start(f32[128,512]{0,1:T(8,128)S(1)} %slice.66), channel_id=1, source_target_pairs={{0,2},{1,3},{2,4},{3,5},{4,6},{5,7},{6,8},{7,9},{8,10},{9,11},{10,... | collective-permute-start | bytes 786440 | tf_op jit(solution)/shard_map/ppermute | solution.py:91
  60.4 11.1 %collective-permute-start.7 = (f32[128,512]{0,1:T(8,128)S(1)}, f32[128,512]{0,1:T(8,128)S(1)}, u32[]{:S(2)}, u32[]{:S(2)}) collective-permute-start(f32[128,512]{0,1:T(8,128)S(1)} %slice.67), channel_id=1, source_target_pairs={{0,14},{1,15},{2,0},{3,1},{4,2},{5,3},{6,4},{7,5},{8,6},{9,7},{10,... | collective-permute-start | bytes 786440 | tf_op jit(solution)/shard_map/ppermute | solution.py:92
  66.0 19.3 %collective-permute-start.10 = (f32[256,512]{0,1:T(8,128)S(1)}, f32[256,512]{0,1:T(8,128)S(1)}, u32[]{:S(2)}, u32[]{:S(2)}) collective-permute-start(f32[256,512]{0,1:T(8,128)S(1)} %collective-permute-done.1), channel_id=1, source_target_pairs={{0,1},{1,0},{2,3},{3,2},{4,5},{5,4},{6,7},{7,6},{8,9},{9,8},{10,11... | collective-permute-start | bytes 1572872 | tf_op jit(solution)/shard_map/ppermute | solution.py:94
  71.5 19.3 %collective-permute-start.14 = (f32[256,512]{0,1:T(8,128)S(1)}, f32[256,512]{0,1:T(8,128)S(1)}, u32[]{:S(2)}, u32[]{:S(2)}) collective-permute-start(f32[256,512]{0,1:T(8,128)S(1)} %collective-permute-done.5), channel_id=1, source_target_pairs={{0,1},{1,0},{2,3},{3,2},{4,5},{5,4},{6,7},{7,6},{8,9},{9,8},{10,11... | collective-permute-start | bytes 1572872 | tf_op jit(solution)/shard_map/ppermute | solution.py:94
  78.2 10.1 %collective-permute-start.11 = (f32[256,512]{0,1:T(8,128)S(1)}, f32[256,512]{0,1:T(8,128)S(1)}, u32[]{:S(2)}, u32[]{:S(2)}) collective-permute-start(f32[256,512]{0,1:T(8,128)S(1)} %collective-permute-done.2), channel_id=1, source_target_pairs={{0,1},{1,0},{2,3},{3,2},{4,5},{5,4},{6,7},{7,6},{8,9},{9,8},{10,11... | collective-permute-start | bytes 1572872 | tf_op jit(solution)/shard_map/ppermute | solution.py:94
  82.2 7.0 %collective-permute-start.12 = (f32[256,512]{0,1:T(8,128)S(1)}, f32[256,512]{0,1:T(8,128)S(1)}, u32[]{:S(2)}, u32[]{:S(2)}) collective-permute-start(f32[256,512]{0,1:T(8,128)S(1)} %constant_dynamic-update-slice_fusion), channel_id=1, source_target_pairs={{0,1},{1,0},{2,3},{3,2},{4,5},{5,4},{6,7},{7,6},{8,9},{9,8},{10,11... | collective-permute-start | bytes 1572872 | tf_op jit(solution)/shard_map/ppermute | solution.py:94
  85.3 4.8 %collective-permute-start.13 = (f32[256,512]{0,1:T(8,128)S(1)}, f32[256,512]{0,1:T(8,128)S(1)}, u32[]{:S(2)}, u32[]{:S(2)}) collective-permute-start(f32[256,512]{0,1:T(8,128)S(1)} %collective-permute-done.6), channel_id=1, source_target_pairs={{0,1},{1,0},{2,3},{3,2},{4,5},{5,4},{6,7},{7,6},{8,9},{9,8},{10,11... | collective-permute-start | bytes 1572872 | tf_op jit(solution)/shard_map/ppermute | solution.py:94
  183.2 3.8 %copy-start = (f32[6,256,512]{2,1,0:T(8,128)S(1)}, f32[6,256,512]{2,1,0:T(8,128)}, u32[]{:S(2)}) copy-start(f32[6,256,512]{2,1,0:T(8,128)} %copy.15) | copy-start | bytes 9437188
  183.2 5.5 %copy-start.1 = (f32[1,256,1536]{2,1,0:T(8,128)S(1)}, f32[1,256,1536]{2,1,0:T(8,128)}, u32[]{:S(2)}) copy-start(f32[1,256,1536]{2,1,0:T(8,128)} %get-tuple-element.12) | copy-start | bytes 4718596
  183.2 5.5 %copy-start.2 = (f32[1,256,1536]{2,1,0:T(8,128)S(1)}, f32[1,256,1536]{2,1,0:T(8,128)}, u32[]{:S(2)}) copy-start(f32[1,256,1536]{2,1,0:T(8,128)} %get-tuple-element.13) | copy-start | bytes 4718596
